TPU v7x, 32 devices: a whole 2x2x4 slice. The times are simulated.
32 devices in a mesh: groups: 2 (over y), ctx: 4 (over z), mp: 2 (over x), sub: 2 (over core).
Axes of the slice: x: 2, y: 2, z: 4, core: 2. Of those that a mesh axis runs over, the one named last changes fastest.
Arguments:
- features: bfloat16 [16384, 3, 4096], P(('groups', 'ctx'), None, ('mp', 'sub')), parts along dimension 0, may hold values from -6 to 6
- short_filter: float32 [7, 3, 4096], P(None, None, ('mp', 'sub')), may hold values from -2 to 2
- mr_filter: bfloat16 [256, 128], P(('mp', 'sub')), may hold values from -0.5 to 0.5
- lr_gates: bfloat16 [16384, 2, 4096], P(('groups', 'ctx'), None, ('mp', 'sub')), parts along dimension 0, may hold values from -6 to 6
- lr_rate: float32 [4096, 16], P(('mp', 'sub')), may hold values from 6.1035156e-05 to 0.05
- lr_residue: float32 [4096, 16], P(('mp', 'sub')), may hold values from -2 to 2
- lr_skip: float32 [4096], P(('mp', 'sub')), may hold values from -3 to 3
Outputs:
- output: bfloat16 [16384, 4096], P(('groups', 'ctx'), ('mp', 'sub')), parts along dimension 0
There are 2 independent parts, one for each index of `groups`. A program takes and returns all parts, laid end to end along the dimension named above; an argument that names none is the same for every part. Nothing has to cross between parts.
All inputs are finite; a program needn't handle non-finite values.
Results may differ from a plain program's by a relative error of at most 0.0059.
Values may be sent and summed in bfloat16 or wider, within the bound.
No kernel may reach another device: no remote copies, remote signals or barrier semaphores. Data moves between devices by JAX's collectives and lax.ppermute only.
A program may use at most 192 MiB of HBM per device.

v0:
```python
import functools

import jax
import jax.numpy as jnp
from jax import lax
from jax.experimental import pallas as pl
from jax.experimental.pallas import tpu as pltpu
from jax.sharding import PartitionSpec as P

TAPS = 128
SHORT = 7
BLOCK = 128
LANES = 1024


def passed_along(shard, axis, by):
    devices = lax.axis_size(axis)
    pairs = [(i, i + by) for i in range(devices) if 0 <= i + by < devices]
    return lax.ppermute(shard, axis, pairs)


def featurize(extended, weights):
    width = weights.shape[0]
    count = extended.shape[0] - (width - 1)
    total = jnp.zeros((count,) + extended.shape[1:], jnp.float32)
    for j in range(width):
        total = total + weights[j] * extended[width - 1 - j : width - 1 - j + count]
    return total


def medium_mix(extended, filters):
    groups, taps = filters.shape
    rows = extended.shape[0] - (taps - 1)
    chans = extended.shape[1]
    padded = jnp.concatenate([jnp.zeros((1, chans), jnp.bfloat16), extended], 0)
    blocks = rows // taps
    before = padded[:rows].reshape(blocks, taps, chans)
    current = padded[taps:].reshape(blocks, taps, chans)
    window = jnp.concatenate([before, current], 1).reshape(
        blocks, 2 * taps, groups, chans // groups
    )
    window = window.transpose(2, 3, 0, 1)
    lag = jnp.arange(taps)[:, None] + taps - jnp.arange(2 * taps)[None, :]
    pick = (lag[None] == jnp.arange(taps)[:, None, None]).astype(jnp.bfloat16)
    toeplitz = jnp.einsum("gj,jts->gts", filters, pick, preferred_element_type=jnp.float32)
    toeplitz = toeplitz.astype(jnp.bfloat16)
    mixed = jnp.einsum("gts,gkbs->gkbt", toeplitz, window, preferred_element_type=jnp.float32)
    return mixed.transpose(2, 3, 0, 1).reshape(rows, chans)


SUB = 16
TERMS = 8


def split_pair(values):
    high = values.astype(jnp.bfloat16)
    low = (values - high.astype(jnp.float32)).astype(jnp.bfloat16)
    return high, low


def carry_subblocks(moments, z, cs_ref, l16, inter_ref=None):
    parts = []
    terms = cs_ref.shape[0]
    modes = z.shape[0]
    for sb in range(moments.shape[0] // terms):
        if inter_ref is not None:
            s = inter_ref[0] * z[0:1]
            for r in range(1, modes):
                s = s + inter_ref[r] * z[r : r + 1]
            parts.append(s)
        acc = cs_ref[0] * moments[sb * terms : sb * terms + 1]
        for n in range(1, terms):
            acc = acc + cs_ref[n] * moments[sb * terms + n : sb * terms + n + 1]
        z = l16 * z + acc
    return z, parts


def state_kernel(x_ref, mom_ref, cs_ref, l16_ref, f_ref, z_ref):
    b = pl.program_id(1)

    @pl.when(b == 0)
    def _():
        z_ref[...] = jnp.zeros_like(z_ref)

    xb = x_ref[...]
    moments = jnp.dot(mom_ref[...], jnp.concatenate([xb, xb], 0), preferred_element_type=jnp.float32)
    z, _ = carry_subblocks(moments, z_ref[...], cs_ref, l16_ref[...])
    z_ref[...] = z

    @pl.when(b == pl.num_programs(1) - 1)
    def _():
        f_ref[...] = z


def main_kernel(x_ref, gate_ref, phi_ref, mom_ref, psi_ref, ci_ref, cs_ref, inter_ref, l16_ref,
                zin_ref, skip_ref, o_ref, z_ref):
    b = pl.program_id(1)

    @pl.when(b == 0)
    def _():
        z_ref[...] = zin_ref[...]

    xb = x_ref[...]
    rows = xb.shape[0]
    x2 = jnp.concatenate([xb, xb], 0)
    near = jnp.dot(phi_ref[...], x2, preferred_element_type=jnp.float32)
    y = ci_ref[0:1] * near[0:rows]
    for n in range(1, ci_ref.shape[0]):
        y = y + ci_ref[n : n + 1] * near[n * rows : (n + 1) * rows]
    moments = jnp.dot(mom_ref[...], x2, preferred_element_type=jnp.float32)
    z, parts = carry_subblocks(moments, z_ref[...], cs_ref, l16_ref[...], inter_ref)
    z_ref[...] = z
    high, low = split_pair(jnp.concatenate(parts, 0))
    far = jnp.dot(psi_ref[...], jnp.concatenate([high, low, high], 0), preferred_element_type=jnp.float32)
    total = y + far + skip_ref[...] * xb.astype(jnp.float32)
    o_ref[...] = (gate_ref[...].astype(jnp.float32) * total).astype(o_ref.dtype)


def bases(rows):
    subs = rows // SUB
    n = jnp.arange(TERMS, dtype=jnp.float32)
    t = jnp.arange(rows)
    sb, tl = t // SUB, (t % SUB).astype(jnp.float32)
    same = sb[:, None] == sb[None, :]
    lag = (t[:, None] - t[None, :]).astype(jnp.float32)
    near = jnp.where(
        (same & (lag >= 0))[None], ((lag - 7.5) / 8.0)[None] ** n[:, None, None], 0.0
    ).reshape(TERMS * rows, rows)
    own = jnp.arange(subs)[:, None] == sb[None, :]
    mom = jnp.where(own[:, None, :], ((7.5 - tl) / 8.0)[None, None, :] ** n[None, :, None], 0.0)
    mom = mom.reshape(subs * TERMS, rows)
    psi = jnp.where(own.T[:, :, None], ((tl - 7.5) / 8.0)[:, None, None] ** n[None, None, :], 0.0)
    psi = psi.reshape(rows, subs * TERMS)
    nh, nl = split_pair(near)
    mh, ml = split_pair(mom)
    ph, pl_ = split_pair(psi)
    return (
        jnp.concatenate([nh, nl], 1),
        jnp.concatenate([mh, ml], 1),
        jnp.concatenate([ph, ph, pl_], 1),
    )


def long_conv_out(lr_input, gate0, lr_rate, lr_residue, lr_skip):
    count, chans = lr_input.shape
    modes = lr_rate.shape[1]
    rows = BLOCK
    lanes = min(LANES, chans)
    blocks = count // rows
    rate = lr_rate.T
    weight = lr_residue.T * jnp.sqrt(rate)
    n = jnp.arange(TERMS, dtype=jnp.float32)
    fact = jnp.cumprod(jnp.maximum(n, 1.0))
    powers = (-8.0 * rate)[None] ** n[:, None, None] / fact[:, None, None]
    l75 = jnp.exp(-7.5 * rate)
    cs = l75[None] * powers
    ci = jnp.sum(weight[None] * cs, axis=1)
    inter = ((weight * jnp.exp(-8.5 * rate))[None] * powers).transpose(1, 0, 2)
    l16 = jnp.exp(-float(SUB) * rate)
    phi, mom, psi = bases(rows)
    grid = (chans // lanes, blocks)
    subs_terms = mom.shape[0]
    params = pltpu.CompilerParams(dimension_semantics=("arbitrary", "arbitrary"))

    final = pl.pallas_call(
        state_kernel,
        grid=grid,
        in_specs=[
            pl.BlockSpec((rows, lanes), lambda j, b: (b, j)),
            pl.BlockSpec((subs_terms, 2 * rows), lambda j, b: (0, 0)),
            pl.BlockSpec((TERMS, modes, lanes), lambda j, b: (0, 0, j)),
            pl.BlockSpec((modes, lanes), lambda j, b: (0, j)),
        ],
        out_specs=pl.BlockSpec((modes, lanes), lambda j, b: (0, j)),
        out_shape=jax.ShapeDtypeStruct((modes, chans), jnp.float32),
        scratch_shapes=[pltpu.VMEM((modes, lanes), jnp.float32)],
        compiler_params=params,
    )(lr_input, mom, cs, l16)

    states = lax.all_gather(final, "ctx")
    devices = states.shape[0]
    me = lax.axis_index("ctx")
    gap = (me - 1 - jnp.arange(devices)).astype(jnp.float32)
    carry = jnp.where(
        (gap >= 0)[:, None, None],
        jnp.exp(-rate[None] * (jnp.maximum(gap, 0.0) * count)[:, None, None]),
        0.0,
    )
    incoming = jnp.sum(carry * states, axis=0)

    return pl.pallas_call(
        main_kernel,
        grid=grid,
        in_specs=[
            pl.BlockSpec((rows, lanes), lambda j, b: (b, j)),
            pl.BlockSpec((rows, lanes), lambda j, b: (b, j)),
            pl.BlockSpec((TERMS * rows, 2 * rows), lambda j, b: (0, 0)),
            pl.BlockSpec((subs_terms, 2 * rows), lambda j, b: (0, 0)),
            pl.BlockSpec((rows, 3 * subs_terms), lambda j, b: (0, 0)),
            pl.BlockSpec((TERMS, lanes), lambda j, b: (0, j)),
            pl.BlockSpec((TERMS, modes, lanes), lambda j, b: (0, 0, j)),
            pl.BlockSpec((modes, TERMS, lanes), lambda j, b: (0, 0, j)),
            pl.BlockSpec((modes, lanes), lambda j, b: (0, j)),
            pl.BlockSpec((modes, lanes), lambda j, b: (0, j)),
            pl.BlockSpec((1, lanes), lambda j, b: (0, j)),
        ],
        out_specs=pl.BlockSpec((rows, lanes), lambda j, b: (b, j)),
        out_shape=jax.ShapeDtypeStruct((count, chans), jnp.bfloat16),
        scratch_shapes=[pltpu.VMEM((modes, lanes), jnp.float32)],
        compiler_params=params,
    )(lr_input, gate0, phi, mom, psi, ci, cs, inter, l16, incoming, lr_skip[None, :])


HALO = 144


def front_kernel(feat_ref, halo_ref, sf_ref, toep_ref, gate_ref, o_ref, ext_ref, prod_ref):
    count = feat_ref.shape[1]
    lanes = feat_ref.shape[2]
    groups = toep_ref.shape[0]
    taps = toep_ref.shape[1]
    width = sf_ref.shape[1]
    for i in range(3):
        ext_ref[i, 0:HALO, :] = halo_ref[i].astype(jnp.float32)
        ext_ref[i, HALO : HALO + count, :] = feat_ref[i].astype(jnp.float32)
    taps_row = [[sf_ref[i, j : j + 1, :] for j in range(width)] for i in range(3)]

    def plane(i, e0):
        total = taps_row[i][0] * ext_ref[i, e0 : e0 + taps, :]
        for j in range(1, width):
            total = total + taps_row[i][j] * ext_ref[i, e0 - j : e0 - j + taps, :]
        return total

    lane_group = lax.broadcasted_iota(jnp.int32, (taps, lanes), 1) // (lanes // groups)
    for t0 in range(-taps, count, taps):
        e0 = t0 + HALO
        prod = (plane(1, e0) * plane(2, e0)).astype(jnp.bfloat16)
        prod_ref[e0 : e0 + taps, :] = prod
        if t0 < 0:
            continue
        window = prod_ref[e0 - taps : e0 + taps, :]
        mixed = None
        for g in range(groups):
            res = jnp.dot(toep_ref[g], window, preferred_element_type=jnp.float32)
            mixed = res if mixed is None else jnp.where(lane_group == g, res, mixed)
        query = plane(0, e0)
        gate = gate_ref[t0 : t0 + taps, :].astype(jnp.float32)
        o_ref[t0 : t0 + taps, :] = (gate * query * mixed).astype(o_ref.dtype)


def front(planes, halo, short_filter, mr_filter, gate1):
    _, count, chans = planes.shape
    groups, taps = mr_filter.shape
    lanes = 128
    per_tile = lanes // (chans // groups)
    lag = jnp.arange(taps)[:, None] + taps - jnp.arange(2 * taps)[None, :]
    pick = (lag[None] == jnp.arange(taps)[:, None, None]).astype(jnp.bfloat16)
    toeplitz = jnp.einsum("gj,jts->gts", mr_filter, pick, preferred_element_type=jnp.float32)
    toeplitz = toeplitz.astype(jnp.bfloat16)
    sf = short_filter.transpose(1, 0, 2)
    width = sf.shape[1]
    return pl.pallas_call(
        front_kernel,
        grid=(chans // lanes,),
        in_specs=[
            pl.BlockSpec((3, count, lanes), lambda j: (0, 0, j)),
            pl.BlockSpec((3, HALO, lanes), lambda j: (0, 0, j)),
            pl.BlockSpec((3, width, lanes), lambda j: (0, 0, j)),
            pl.BlockSpec((per_tile, taps, 2 * taps), lambda j: (j, 0, 0)),
            pl.BlockSpec((count, lanes), lambda j: (0, j)),
        ],
        out_specs=pl.BlockSpec((count, lanes), lambda j: (0, j)),
        out_shape=jax.ShapeDtypeStruct((count, chans), jnp.bfloat16),
        scratch_shapes=[
            pltpu.VMEM((3, HALO + count, lanes), jnp.float32),
            pltpu.VMEM((HALO + count, lanes), jnp.bfloat16),
        ],
        compiler_params=pltpu.CompilerParams(dimension_semantics=("arbitrary",)),
    )(planes, halo, sf, toeplitz, gate1)


def per_device(features, short_filter, mr_filter, lr_gates, lr_rate, lr_residue, lr_skip):
    count = features.shape[0]
    planes = features.transpose(1, 0, 2)
    halo = passed_along(planes[:, count - HALO :], "ctx", 1)
    gates = lr_gates.transpose(1, 0, 2)
    lr_input = front(planes, halo, short_filter, mr_filter, gates[1])
    return long_conv_out(lr_input, gates[0], lr_rate, lr_residue, lr_skip)


def solution(mesh):
    in_specs = (
        P(("groups", "ctx"), None, ("mp", "sub")),
        P(None, None, ("mp", "sub")),
        P(("mp", "sub"), None),
        P(("groups", "ctx"), None, ("mp", "sub")),
        P(("mp", "sub"), None),
        P(("mp", "sub"), None),
        P(("mp", "sub")),
    )
    out_specs = P(("groups", "ctx"), ("mp", "sub"))
    return jax.shard_map(
        per_device, mesh=mesh, in_specs=in_specs, out_specs=out_specs, check_vma=False
    )
```

profile of v0, /device:TPU:0, one launch (start us, length us, event | category | flops | bytes accessed | tf_op | source)
XLA Modules:
  0.0 128.0 jit_solution(16361854772936569014)
XLA Ops:
  0.0 0.0 copy-start
  0.0 1.2 slice.12
  1.2 5.0 %collective-permute-start = (bf16[3,144,1024]{2,1,0:T(8,128)(2,1)S(1)}, bf16[3,144,1024]{2,1,0:T(8,128)(2,1)S(1)}, u32[]{:S(2)}, u32[]{:S(2)}) collective-permute-start(bf16[3,144,1024]{2,1,0:T(8,128)(2,1)S(1)} %slice.12), channel_id=1, source_target_pairs={{0,4},{4,8},{8,12},{1,5},{5,9},{9,13},{2,6},{6,10},{10,14},{3,7},{... | collective-permute-start | bytes 2654216 | tf_op jit(solution)/shard_map/ppermute | solution.py:19
  6.5 0.1 fusion.7
  6.6 1.5 %negate_bitcast_fusion = (f32[16,1024]{1,0:T(8,128)S(1)}, f32[16,1024]{1,0:T(8,128)S(1)}, f32[16,1024]{1,0:T(8,128)S(1)}, f32[16,1024]{1,0:T(8,128)S(1)}, f32[16,1024]{1,0:T(8,128)}) fusion(f32[1024,16]{0,1:T(8,128)} %param.11, f32[1024,16]{0,1:T(8,128)} %param.12), kind=kLoop, calls=%fused_computation.21 | loop fusion | flops 81920 | bytes 458752 | tf_op jit(solution)/shard_map/neg | solution.py:186
  8.1 0.9 bitcast_multiply_fusion
  9.0 0.1 iota_subtract_fusion
  9.1 0.1 copy.18
  9.3 0.1 copy.17
  9.4 0.2 reduce-window.8
  9.6 1.4 %divide_multiply_fusion.inter_ref = f32[16,8,1024]{2,1,0:T(8,128)} fusion(f32[8]{0:T(128)S(1)} %bitcast.71, f32[16,1024]{1,0:T(8,128)S(1)} %get-tuple-element.12, f32[16,1024]{1,0:T(8,128)S(1)} %bitcast_multiply_fusion), kind=kLoop, calls=%fused_computation.14 | loop fusion | flops 262144 | bytes 655392 | tf_op jit(solution)/shard_map/mul | solution.py:158
  10.9 1.6 %divide_multiply_fusion.1 = (f32[8,16,1024]{2,1,0:T(8,128)}, f32[8,1024]{1,0:T(8,128)}) fusion(f32[8]{0:T(128)S(1)} %bitcast.72, f32[16,1024]{1,0:T(8,128)S(1)} %get-tuple-element.12, f32[16,1024]{1,0:T(8,128)S(1)} %get-tuple-element.13, f32[16,1024]{1,0:T(8,128)S(1)} %get-tuple-element.14), kind=kLoop, calls=%fused_computation.16 | loop fusion | flops 516096 | bytes 753696 | tf_op jit(solution)/shard_map/mul | solution.py:156
  12.5 0.6 pad_maximum_fusion.2.mom_ref
  13.1 0.0 copy-done
  13.1 3.9 %fusion = bf16[128,256,64]{1,2,0:T(8,128)(2,1)S(1)} fusion(s32[128,256]{1,0:T(8,128)S(1)} %iota_subtract_fusion, bf16[64,128]{1,0:T(8,128)(2,1)S(1)} %copy-done), kind=kOutput, calls=%fused_computation.1 | convolution fusion | flops 541065216 | bytes 4341760 | tf_op jit(solution)/shard_map/gj,jts->gts/dot_general | solution.py:258
  17.1 1.0 fusion.5
  18.1 0.9 pad_maximum_fusion.phi_ref
  19.0 9.3 %copy.24 = bf16[2048,2,1024]{2,0,1:T(8,128)(2,1)} copy(bf16[2048,2,1024]{2,1,0:T(2,128)(2,1)} %param.10) | data formatting | bytes 16777216 | tf_op args[3]
  28.2 0.0 copy-start.1
  28.2 4.4 %copy.25 = bf16[128,256,64]{1,0,2:T(8,128)(2,1)} copy(bf16[128,256,64]{1,2,0:T(8,128)(2,1)S(1)} %fusion) | data formatting | bytes 8388608 | tf_op jit(solution)/shard_map/gj,jts->gts/dot_general | solution.py:258
  32.7 0.7 pad_maximum_fusion.1.psi_ref
  33.4 0.0 copy-done.1
  33.4 3.7 %slice_bitcast_fusion = (bf16[2048,1024]{1,0:T(8,128)(2,1)}, bf16[2048,1024]{1,0:T(8,128)(2,1)}) fusion(bf16[2,2048,1024]{2,1,0:T(8,128)(2,1)S(1)} %bitcast.64), kind=kLoop, calls=%fused_computation.6 | loop fusion | bytes 16777216 | tf_op jit(solution)/shard_map/squeeze | solution.py:288
  37.1 0.0 collective-permute-done.halo_ref
  37.1 0.0 copy-start.2
  37.1 1.0 copy-done.2
  38.1 30.0 %shard_map.73.x_ref = bf16[2048,1024]{1,0:T(8,128)(2,1)} custom-call(bf16[3,2048,1024]{2,1,0:T(8,128)(2,1)} %bitcast.67, bf16[3,144,1024]{2,1,0:T(8,128)(2,1)} %copy-done.2, f32[3,7,1024]{2,1,0:T(8,128)} %bitcast.69, bf16[64,128,256]{2,1,0:T(8,128)(2,1)} %bitcast.65, bf16[2048,1024]{1,0:T(8,128)(2,1)} %get-tuple-element.6.gate_ref), custom_call_target="tpu_custom_call" | custom-call | tf_op jit(solution)/shard_map/pallas_call | solution.py:262
  68.0 13.3 %shard_map.74 = f32[16,1024]{1,0:T(8,128)} custom-call(bf16[2048,1024]{1,0:T(8,128)(2,1)} %shard_map.73.x_ref, bf16[64,256]{1,0:T(8,128)(2,1)} %pad_maximum_fusion.2.mom_ref, f32[8,16,1024]{2,1,0:T(8,128)} %get-tuple-element.7.cs_ref, f32[16,1024]{1,0:T(8,128)} %get-tuple-element.15.l16_ref), custom_call_target="tpu_custom_call" | custom-call | tf_op jit(solution)/shard_map/pallas_call | solution.py:165
  81.4 14.9 %all-gather = f32[64,1024]{1,0:T(8,128)S(1)} all-gather(f32[16,1024]{1,0:T(8,128)} %shard_map.74), channel_id=2, replica_groups=mesh['groups'=2,'ctx'=4,'mp'=2,'sub'=2] {'ctx'}, dimensions={0}, use_global_device_ids=true | all-gather | bytes 327680 | tf_op jit(solution)/shard_map/all_gather | solution.py:180
  96.3 0.8 multiply_reduce_fusion.1.zin_ref
  97.0 30.9 %shard_map.75 = bf16[2048,1024]{1,0:T(8,128)(2,1)} custom-call(bf16[2048,1024]{1,0:T(8,128)(2,1)} %shard_map.73.x_ref, bf16[2048,1024]{1,0:T(8,128)(2,1)} %get-tuple-element.5.gate_ref, bf16[1024,256]{1,0:T(8,128)(2,1)} %pad_maximum_fusion.phi_ref, bf16[64,256]{1,0:T(8,128)(2,1)} %pad_maximum_fusion.2.mom_ref, bf16[128,192]{1,0:T(8,128)(2,1)} %pad_maximum_fusion.1.psi_ref, ...), custom_call_target="tpu_custom_call" | custom-call | tf_op jit(solution)/shard_map/pallas_call | solution.py:191
  (18 shorter events, 0.2 us)
Async XLA Ops:
  0.0 13.1 %copy-start = (bf16[64,128]{1,0:T(8,128)(2,1)S(1)}, bf16[64,128]{1,0:T(8,128)(2,1)}, u32[]{:S(2)}) copy-start(bf16[64,128]{1,0:T(8,128)(2,1)} %param.9) | copy-start | bytes 49156
  1.2 35.9 %collective-permute-start = (bf16[3,144,1024]{2,1,0:T(8,128)(2,1)S(1)}, bf16[3,144,1024]{2,1,0:T(8,128)(2,1)S(1)}, u32[]{:S(2)}, u32[]{:S(2)}) collective-permute-start(bf16[3,144,1024]{2,1,0:T(8,128)(2,1)S(1)} %slice.12), channel_id=1, source_target_pairs={{0,4},{4,8},{8,12},{1,5},{5,9},{9,13},{2,6},{6,10},{10,14},{3,7},{... | collective-permute-start | bytes 2654216 | tf_op jit(solution)/shard_map/ppermute | solution.py:19
  28.2 5.2 %copy-start.1 = (bf16[2048,2,1024]{2,0,1:T(8,128)(2,1)S(1)}, bf16[2048,2,1024]{2,0,1:T(8,128)(2,1)}, u32[]{:S(2)}) copy-start(bf16[2048,2,1024]{2,0,1:T(8,128)(2,1)} %copy.24) | copy-start | bytes 25165828
  37.1 1.0 copy-start.2
where the time goes:
time: 129 us; the launch traced here: 128 us
  Pallas kernels  74.2 us (58%)
  local copies, waits for them, and re-layouts  19.9 us (15%)
  blocking collectives  14.9 us (12%)
  other arithmetic  9.82 us (8%)
  starting transfers between devices  5.01 us (4%)
  matrix products  3.93 us (3%)
    pallas_call x1, Pallas kernels, long_conv_out(): pl.pallas_call(main_kernel, grid=grid, in_specs=[pl.BlockSpec((rows, lane...  30.9 us
    pallas_call x1, Pallas kernels, front(): pl.pallas_call(front_kernel, grid=(chans // lanes,), in_specs=[pl.BlockSp...  30 us
    all_gather x1, blocking collectives, long_conv_out(): states = lax.all_gather(final, 'ctx')  14.9 us
    pallas_call x1, Pallas kernels, long_conv_out(): pl.pallas_call(state_kernel, grid=grid, in_specs=[pl.BlockSpec((rows, lan...  13.3 us
    unnamed x7, local copies, waits for them, and re-layouts  10.3 us
    ppermute x1, starting transfers between devices, passed_along(): return lax.ppermute(shard, axis, pairs)  5.01 us
    dot_general x1, local copies, waits for them, and re-layouts, front(): jnp.einsum('gj,jts->gts', mr_filter, pick, preferred_element_type=jnp.flo...  4.43 us
    dot_general x1, matrix products, front(): jnp.einsum('gj,jts->gts', mr_filter, pick, preferred_element_type=jnp.flo...  3.93 us
  transfers between devices with their start and end apart: 1, of which 0 were waited for; matrix products, arithmetic and copies ran while one was open for 24% of the time, Pallas kernels for 0%

commit v1 on v0

--- a/solution.py
+++ b/solution.py
@@ -11,6 +11,7 @@
 SHORT = 7
 BLOCK = 128
 LANES = 1024
+FRONT_LANES = 512
 
 
 def passed_along(shard, axis, by):
@@ -231,7 +232,9 @@
             total = total + taps_row[i][j] * ext_ref[i, e0 - j : e0 - j + taps, :]
         return total
 
-    lane_group = lax.broadcasted_iota(jnp.int32, (taps, lanes), 1) // (lanes // groups)
+    chunk = 128
+    per_chunk = groups * chunk // lanes
+    lane_group = lax.broadcasted_iota(jnp.int32, (taps, chunk), 1) // (chunk // per_chunk)
     for t0 in range(-taps, count, taps):
         e0 = t0 + HALO
         prod = (plane(1, e0) * plane(2, e0)).astype(jnp.bfloat16)
@@ -239,10 +242,15 @@
         if t0 < 0:
             continue
         window = prod_ref[e0 - taps : e0 + taps, :]
-        mixed = None
-        for g in range(groups):
-            res = jnp.dot(toep_ref[g], window, preferred_element_type=jnp.float32)
-            mixed = res if mixed is None else jnp.where(lane_group == g, res, mixed)
+        pieces = []
+        for q in range(lanes // chunk):
+            part = window[:, q * chunk : (q + 1) * chunk]
+            mixed = None
+            for g in range(per_chunk):
+                res = jnp.dot(toep_ref[q * per_chunk + g], part, preferred_element_type=jnp.float32)
+                mixed = res if mixed is None else jnp.where(lane_group == g, res, mixed)
+            pieces.append(mixed)
+        mixed = pieces[0] if len(pieces) == 1 else jnp.concatenate(pieces, 1)
         query = plane(0, e0)
         gate = gate_ref[t0 : t0 + taps, :].astype(jnp.float32)
         o_ref[t0 : t0 + taps, :] = (gate * query * mixed).astype(o_ref.dtype)
@@ -251,7 +259,7 @@
 def front(planes, halo, short_filter, mr_filter, gate1):
     _, count, chans = planes.shape
     groups, taps = mr_filter.shape
-    lanes = 128
+    lanes = min(FRONT_LANES, chans)
     per_tile = lanes // (chans // groups)
     lag = jnp.arange(taps)[:, None] + taps - jnp.arange(2 * taps)[None, :]
     pick = (lag[None] == jnp.arange(taps)[:, None, None]).astype(jnp.bfloat16)

time: 129 us -> 140 us (1.085)
  Pallas kernels: 74.2 us -> 86.1 us
    pallas_call x1, Pallas kernels: 30 us -> 41.9 us  [front(): pl.pallas_call(front_kernel, grid=(chans // lanes,), in_specs=[pl.BlockSp...]
  transfers between devices with their start and end apart: 1 -> 1, of which waited for: 0 -> 0; matrix products, arithmetic and copies ran while one was open for 24% -> 22% of each run, Pallas kernels for 0% -> 0%
where the time goes in v1:
time: 140 us
  Pallas kernels  86.1 us (62%)
  local copies, waits for them, and re-layouts  19.9 us (14%)
  blocking collectives  14.9 us (11%)
  other arithmetic  9.82 us (7%)
  starting transfers between devices  5.01 us (4%)
  matrix products  3.93 us (3%)
    pallas_call x1, Pallas kernels, front(): pl.pallas_call(front_kernel, grid=(chans // lanes,), in_specs=[pl.BlockSp...  41.9 us
    pallas_call x1, Pallas kernels, long_conv_out(): pl.pallas_call(main_kernel, grid=grid, in_specs=[pl.BlockSpec((rows, lane...  30.9 us
    all_gather x1, blocking collectives, long_conv_out(): states = lax.all_gather(final, 'ctx')  14.9 us
    pallas_call x1, Pallas kernels, long_conv_out(): pl.pallas_call(state_kernel, grid=grid, in_specs=[pl.BlockSpec((rows, lan...  13.3 us
    unnamed x7, local copies, waits for them, and re-layouts  10.3 us
    ppermute x1, starting transfers between devices, passed_along(): return lax.ppermute(shard, axis, pairs)  5.01 us
    dot_general x1, local copies, waits for them, and re-layouts, front(): jnp.einsum('gj,jts->gts', mr_filter, pick, preferred_element_type=jnp.flo...  4.43 us
    dot_general x1, matrix products, front(): jnp.einsum('gj,jts->gts', mr_filter, pick, preferred_element_type=jnp.flo...  3.93 us
  transfers between devices with their start and end apart: 1, of which 0 were waited for; matrix products, arithmetic and copies ran while one was open for 22% of the time, Pallas kernels for 0%

profile of v1, /device:TPU:0, one launch (start us, length us, event | category | flops | bytes accessed | tf_op | source)
XLA Modules:
  0.0 139.9 jit_solution(11735459553704311397)
XLA Ops:
  0.0 0.0 copy-start
  0.0 1.2 slice.12
  1.2 5.0 %collective-permute-start = (bf16[3,144,1024]{2,1,0:T(8,128)(2,1)S(1)}, bf16[3,144,1024]{2,1,0:T(8,128)(2,1)S(1)}, u32[]{:S(2)}, u32[]{:S(2)}) collective-permute-start(bf16[3,144,1024]{2,1,0:T(8,128)(2,1)S(1)} %slice.12), channel_id=1, source_target_pairs={{0,4},{4,8},{8,12},{1,5},{5,9},{9,13},{2,6},{6,10},{10,14},{3,7},{... | collective-permute-start | bytes 2654216 | tf_op jit(solution)/shard_map/ppermute | solution.py:20
  6.5 0.1 fusion.7
  6.6 1.5 %negate_bitcast_fusion = (f32[16,1024]{1,0:T(8,128)S(1)}, f32[16,1024]{1,0:T(8,128)S(1)}, f32[16,1024]{1,0:T(8,128)S(1)}, f32[16,1024]{1,0:T(8,128)S(1)}, f32[16,1024]{1,0:T(8,128)}) fusion(f32[1024,16]{0,1:T(8,128)} %param.11, f32[1024,16]{0,1:T(8,128)} %param.12), kind=kLoop, calls=%fused_computation.21 | loop fusion | flops 81920 | bytes 458752 | tf_op jit(solution)/shard_map/neg | solution.py:187
  8.1 0.9 bitcast_multiply_fusion
  9.0 0.1 iota_subtract_fusion
  9.1 0.1 copy.18
  9.3 0.1 copy.17
  9.4 0.2 reduce-window.8
  9.6 1.4 divide_multiply_fusion.inter_ref
  10.9 1.6 %divide_multiply_fusion.1 = (f32[8,16,1024]{2,1,0:T(8,128)}, f32[8,1024]{1,0:T(8,128)}) fusion(f32[8]{0:T(128)S(1)} %bitcast.72, f32[16,1024]{1,0:T(8,128)S(1)} %get-tuple-element.12, f32[16,1024]{1,0:T(8,128)S(1)} %get-tuple-element.13, f32[16,1024]{1,0:T(8,128)S(1)} %get-tuple-element.14), kind=kLoop, calls=%fused_computation.16 | loop fusion | flops 516096 | bytes 753696 | tf_op jit(solution)/shard_map/mul | solution.py:157
  12.5 0.6 pad_maximum_fusion.2.mom_ref
  13.1 0.0 copy-done
  13.1 3.9 %fusion = bf16[128,256,64]{1,2,0:T(8,128)(2,1)S(1)} fusion(s32[128,256]{1,0:T(8,128)S(1)} %iota_subtract_fusion, bf16[64,128]{1,0:T(8,128)(2,1)S(1)} %copy-done), kind=kOutput, calls=%fused_computation.1 | convolution fusion | flops 541065216 | bytes 4341760 | tf_op jit(solution)/shard_map/gj,jts->gts/dot_general | solution.py:266
  17.1 1.0 fusion.5
  18.1 0.9 pad_maximum_fusion.phi_ref
  19.0 9.3 %copy.24 = bf16[2048,2,1024]{2,0,1:T(8,128)(2,1)} copy(bf16[2048,2,1024]{2,1,0:T(2,128)(2,1)} %param.10) | data formatting | bytes 16777216 | tf_op args[3]
  28.2 0.0 copy-start.1
  28.2 4.4 %copy.25 = bf16[128,256,64]{1,0,2:T(8,128)(2,1)} copy(bf16[128,256,64]{1,2,0:T(8,128)(2,1)S(1)} %fusion) | data formatting | bytes 8388608 | tf_op jit(solution)/shard_map/gj,jts->gts/dot_general | solution.py:266
  32.7 0.7 pad_maximum_fusion.1.psi_ref
  33.4 0.0 copy-done.1
  33.4 3.7 %slice_bitcast_fusion = (bf16[2048,1024]{1,0:T(8,128)(2,1)}, bf16[2048,1024]{1,0:T(8,128)(2,1)}) fusion(bf16[2,2048,1024]{2,1,0:T(8,128)(2,1)S(1)} %bitcast.64), kind=kLoop, calls=%fused_computation.6 | loop fusion | bytes 16777216 | tf_op jit(solution)/shard_map/squeeze | solution.py:296
  37.1 0.0 collective-permute-done.halo_ref
  37.1 0.0 copy-start.2
  37.1 1.0 copy-done.2
  38.1 41.9 %shard_map.73.x_ref = bf16[2048,1024]{1,0:T(8,128)(2,1)} custom-call(bf16[3,2048,1024]{2,1,0:T(8,128)(2,1)} %bitcast.67, bf16[3,144,1024]{2,1,0:T(8,128)(2,1)} %copy-done.2, f32[3,7,1024]{2,1,0:T(8,128)} %bitcast.69, bf16[64,128,256]{2,1,0:T(8,128)(2,1)} %bitcast.65, bf16[2048,1024]{1,0:T(8,128)(2,1)} %get-tuple-element.6.gate_ref), custom_call_target="tpu_custom_call" | custom-call | tf_op jit(solution)/shard_map/pallas_call | solution.py:270
  80.0 13.3 %shard_map.74 = f32[16,1024]{1,0:T(8,128)} custom-call(bf16[2048,1024]{1,0:T(8,128)(2,1)} %shard_map.73.x_ref, bf16[64,256]{1,0:T(8,128)(2,1)} %pad_maximum_fusion.2.mom_ref, f32[8,16,1024]{2,1,0:T(8,128)} %get-tuple-element.7.cs_ref, f32[16,1024]{1,0:T(8,128)} %get-tuple-element.15.l16_ref), custom_call_target="tpu_custom_call" | custom-call | tf_op jit(solution)/shard_map/pallas_call | solution.py:166
  93.3 14.9 %all-gather = f32[64,1024]{1,0:T(8,128)S(1)} all-gather(f32[16,1024]{1,0:T(8,128)} %shard_map.74), channel_id=2, replica_groups=mesh['groups'=2,'ctx'=4,'mp'=2,'sub'=2] {'ctx'}, dimensions={0}, use_global_device_ids=true | all-gather | bytes 327680 | tf_op jit(solution)/shard_map/all_gather | solution.py:181
  108.2 0.8 multiply_reduce_fusion.1.zin_ref
  109.0 30.9 %shard_map.75 = bf16[2048,1024]{1,0:T(8,128)(2,1)} custom-call(bf16[2048,1024]{1,0:T(8,128)(2,1)} %shard_map.73.x_ref, bf16[2048,1024]{1,0:T(8,128)(2,1)} %get-tuple-element.5.gate_ref, bf16[1024,256]{1,0:T(8,128)(2,1)} %pad_maximum_fusion.phi_ref, bf16[64,256]{1,0:T(8,128)(2,1)} %pad_maximum_fusion.2.mom_ref, bf16[128,192]{1,0:T(8,128)(2,1)} %pad_maximum_fusion.1.psi_ref, ...), custom_call_target="tpu_custom_call" | custom-call | tf_op jit(solution)/shard_map/pallas_call | solution.py:192
  (18 shorter events, 0.2 us)
Async XLA Ops:
  0.0 13.1 %copy-start = (bf16[64,128]{1,0:T(8,128)(2,1)S(1)}, bf16[64,128]{1,0:T(8,128)(2,1)}, u32[]{:S(2)}) copy-start(bf16[64,128]{1,0:T(8,128)(2,1)} %param.9) | copy-start | bytes 49156
  1.2 35.9 %collective-permute-start = (bf16[3,144,1024]{2,1,0:T(8,128)(2,1)S(1)}, bf16[3,144,1024]{2,1,0:T(8,128)(2,1)S(1)}, u32[]{:S(2)}, u32[]{:S(2)}) collective-permute-start(bf16[3,144,1024]{2,1,0:T(8,128)(2,1)S(1)} %slice.12), channel_id=1, source_target_pairs={{0,4},{4,8},{8,12},{1,5},{5,9},{9,13},{2,6},{6,10},{10,14},{3,7},{... | collective-permute-start | bytes 2654216 | tf_op jit(solution)/shard_map/ppermute | solution.py:20
  28.2 5.2 %copy-start.1 = (bf16[2048,2,1024]{2,0,1:T(8,128)(2,1)S(1)}, bf16[2048,2,1024]{2,0,1:T(8,128)(2,1)}, u32[]{:S(2)}) copy-start(bf16[2048,2,1024]{2,0,1:T(8,128)(2,1)} %copy.24) | copy-start | bytes 25165828
  37.1 1.0 copy-start.2

commit v2 on v0

--- a/solution.py
+++ b/solution.py
@@ -113,7 +113,7 @@
     high, low = split_pair(jnp.concatenate(parts, 0))
     far = jnp.dot(psi_ref[...], jnp.concatenate([high, low, high], 0), preferred_element_type=jnp.float32)
     total = y + far + skip_ref[...] * xb.astype(jnp.float32)
-    o_ref[...] = (gate_ref[...].astype(jnp.float32) * total).astype(o_ref.dtype)
+    o_ref[...] = (gate_ref[:, 0, :].astype(jnp.float32) * total).astype(o_ref.dtype)
 
 
 def bases(rows):
@@ -193,7 +193,7 @@
         grid=grid,
         in_specs=[
             pl.BlockSpec((rows, lanes), lambda j, b: (b, j)),
-            pl.BlockSpec((rows, lanes), lambda j, b: (b, j)),
+            pl.BlockSpec((rows, 2, lanes), lambda j, b: (b, 0, j)),
             pl.BlockSpec((TERMS * rows, 2 * rows), lambda j, b: (0, 0)),
             pl.BlockSpec((subs_terms, 2 * rows), lambda j, b: (0, 0)),
             pl.BlockSpec((rows, 3 * subs_terms), lambda j, b: (0, 0)),
@@ -214,12 +214,18 @@
 HALO = 144
 
 
-def front_kernel(feat_ref, halo_ref, sf_ref, toep_ref, gate_ref, o_ref, ext_ref, prod_ref):
+def front_kernel(feat_ref, halo_ref, sf_ref, rows_ref, gate_ref, o_ref, ext_ref, prod_ref):
     count = feat_ref.shape[1]
     lanes = feat_ref.shape[2]
-    groups = toep_ref.shape[0]
-    taps = toep_ref.shape[1]
+    groups = rows_ref.shape[0]
+    taps = rows_ref.shape[1] // 2
     width = sf_ref.shape[1]
+    toep = [
+        pltpu.roll(
+            jnp.broadcast_to(rows_ref[g : g + 1, :], (taps, 2 * taps)), 0, 1, stride=1, stride_axis=0
+        ).astype(jnp.bfloat16)
+        for g in range(groups)
+    ]
     for i in range(3):
         ext_ref[i, 0:HALO, :] = halo_ref[i].astype(jnp.float32)
         ext_ref[i, HALO : HALO + count, :] = feat_ref[i].astype(jnp.float32)
@@ -241,22 +247,26 @@
         window = prod_ref[e0 - taps : e0 + taps, :]
         mixed = None
         for g in range(groups):
-            res = jnp.dot(toep_ref[g], window, preferred_element_type=jnp.float32)
+            res = jnp.dot(toep[g], window, preferred_element_type=jnp.float32)
             mixed = res if mixed is None else jnp.where(lane_group == g, res, mixed)
         query = plane(0, e0)
-        gate = gate_ref[t0 : t0 + taps, :].astype(jnp.float32)
+        gate = gate_ref[t0 : t0 + taps, 1, :].astype(jnp.float32)
         o_ref[t0 : t0 + taps, :] = (gate * query * mixed).astype(o_ref.dtype)
 
 
-def front(planes, halo, short_filter, mr_filter, gate1):
+def front(planes, halo, short_filter, mr_filter, gates):
     _, count, chans = planes.shape
     groups, taps = mr_filter.shape
     lanes = 128
     per_tile = lanes // (chans // groups)
-    lag = jnp.arange(taps)[:, None] + taps - jnp.arange(2 * taps)[None, :]
-    pick = (lag[None] == jnp.arange(taps)[:, None, None]).astype(jnp.bfloat16)
-    toeplitz = jnp.einsum("gj,jts->gts", mr_filter, pick, preferred_element_type=jnp.float32)
-    toeplitz = toeplitz.astype(jnp.bfloat16)
+    template = jnp.concatenate(
+        [
+            jnp.zeros((groups, 1), jnp.float32),
+            mr_filter[:, ::-1].astype(jnp.float32),
+            jnp.zeros((groups, taps - 1), jnp.float32),
+        ],
+        1,
+    )
     sf = short_filter.transpose(1, 0, 2)
     width = sf.shape[1]
     return pl.pallas_call(
@@ -266,8 +276,8 @@
             pl.BlockSpec((3, count, lanes), lambda j: (0, 0, j)),
             pl.BlockSpec((3, HALO, lanes), lambda j: (0, 0, j)),
             pl.BlockSpec((3, width, lanes), lambda j: (0, 0, j)),
-            pl.BlockSpec((per_tile, taps, 2 * taps), lambda j: (j, 0, 0)),
-            pl.BlockSpec((count, lanes), lambda j: (0, j)),
+            pl.BlockSpec((per_tile, 2 * taps), lambda j: (j, 0)),
+            pl.BlockSpec((count, 2, lanes), lambda j: (0, 0, j)),
         ],
         out_specs=pl.BlockSpec((count, lanes), lambda j: (0, j)),
         out_shape=jax.ShapeDtypeStruct((count, chans), jnp.bfloat16),
@@ -276,16 +286,15 @@
             pltpu.VMEM((HALO + count, lanes), jnp.bfloat16),
         ],
         compiler_params=pltpu.CompilerParams(dimension_semantics=("arbitrary",)),
-    )(planes, halo, sf, toeplitz, gate1)
+    )(planes, halo, sf, template, gates)
 
 
 def per_device(features, short_filter, mr_filter, lr_gates, lr_rate, lr_residue, lr_skip):
     count = features.shape[0]
     planes = features.transpose(1, 0, 2)
     halo = passed_along(planes[:, count - HALO :], "ctx", 1)
-    gates = lr_gates.transpose(1, 0, 2)
-    lr_input = front(planes, halo, short_filter, mr_filter, gates[1])
-    return long_conv_out(lr_input, gates[0], lr_rate, lr_residue, lr_skip)
+    lr_input = front(planes, halo, short_filter, mr_filter, lr_gates)
+    return long_conv_out(lr_input, lr_gates, lr_rate, lr_residue, lr_skip)
 
 
 def solution(mesh):

time: 129 us -> 129 us (level)
  local copies, waits for them, and re-layouts: 19.9 us -> 3.28 us
  Pallas kernels: 74.2 us -> 86.7 us
  waiting for transfers between devices: 0.01 us -> 7.87 us
  matrix products: 3.93 us -> 0 us
    pallas_call x1, Pallas kernels: 30 us -> 40.5 us  [front(): pl.pallas_call(front_kernel, grid=(chans // lanes,), in_specs=[pl.BlockSp...]
    unnamed x7 -> x2, local copies, waits for them, and re-layouts: 10.3 us -> 0.91 us
    ppermute x1, waiting for transfers between devices: 0.01 us -> 7.87 us  [passed_along(): return lax.ppermute(shard, axis, pairs)]
    dot_general x1 -> x0, local copies, waits for them, and re-layouts: 4.43 us -> none  [front(): jnp.einsum('gj,jts->gts', mr_filter, pick, preferred_element_type=jnp.flo...]
    dot_general x1 -> x0, matrix products: 3.93 us -> none  [front(): jnp.einsum('gj,jts->gts', mr_filter, pick, preferred_element_type=jnp.flo...]
    squeeze x1 -> x0, local copies, waits for them, and re-layouts: 3.72 us -> none  [per_device(): return long_conv_out(lr_input, gates[0], lr_rate, lr_residue, lr_skip)]
    pallas_call x1, Pallas kernels: 30.9 us -> 32.9 us  [long_conv_out(): pl.pallas_call(main_kernel, grid=grid, in_specs=[pl.BlockSpec((rows, lane...]
  transfers between devices with their start and end apart: 1 -> 1, of which waited for: 0 -> 1; matrix products, arithmetic and copies ran while one was open for 24% -> 8% of each run, Pallas kernels for 0% -> 0%
where the time goes in v2:
time: 129 us
  Pallas kernels  86.7 us (67%)
  blocking collectives  15.2 us (12%)
  other arithmetic  10.4 us (8%)
  waiting for transfers between devices  7.87 us (6%)
  starting transfers between devices  5.01 us (4%)
  local copies, waits for them, and re-layouts  3.28 us (3%)
    pallas_call x1, Pallas kernels, front(): pl.pallas_call(front_kernel, grid=(chans // lanes,), in_specs=[pl.BlockSp...  40.5 us
    pallas_call x1, Pallas kernels, long_conv_out(): pl.pallas_call(main_kernel, grid=grid, in_specs=[pl.BlockSpec((rows, lane...  32.9 us
    all_gather x1, blocking collectives, long_conv_out(): states = lax.all_gather(final, 'ctx')  15.2 us
    pallas_call x1, Pallas kernels, long_conv_out(): pl.pallas_call(state_kernel, grid=grid, in_specs=[pl.BlockSpec((rows, lan...  13.3 us
    ppermute x1, waiting for transfers between devices, passed_along(): return lax.ppermute(shard, axis, pairs)  7.87 us
    ppermute x1, starting transfers between devices, passed_along(): return lax.ppermute(shard, axis, pairs)  5.01 us
  transfers between devices with their start and end apart: 1, of which 1 were waited for; matrix products, arithmetic and copies ran while one was open for 8% of the time, Pallas kernels for 0%

profile of v2, /device:TPU:0, one launch (start us, length us, event | category | flops | bytes accessed | tf_op | source)
XLA Modules:
  0.0 128.6 jit_solution(4795033342562745494)
XLA Ops:
  0.0 1.2 slice.4
  1.2 5.0 %collective-permute-start = (bf16[3,144,1024]{2,1,0:T(8,128)(2,1)S(1)}, bf16[3,144,1024]{2,1,0:T(8,128)(2,1)S(1)}, u32[]{:S(2)}, u32[]{:S(2)}) collective-permute-start(bf16[3,144,1024]{2,1,0:T(8,128)(2,1)S(1)} %slice.4), channel_id=1, source_target_pairs={{0,4},{4,8},{8,12},{1,5},{5,9},{9,13},{2,6},{6,10},{10,14},{3,7},{... | collective-permute-start | bytes 2654216 | tf_op jit(solution)/shard_map/ppermute | solution.py:19
  6.4 0.1 fusion.4
  6.6 0.1 pad.9.clone
  6.7 0.1 copy.12
  6.8 0.8 rev.3
  7.6 0.1 copy.11
  7.7 0.7 pad_maximum_fusion.1.psi_ref
  8.4 0.6 pad_maximum_fusion.2.mom_ref
  9.1 0.9 bitcast_multiply_fusion
  10.0 0.7 maximum_maximum_fusion.rows_ref
  10.7 0.2 reduce-window.8
  10.9 1.0 fusion.2
  11.9 0.9 pad_maximum_fusion.phi_ref
  12.7 1.5 %negate_bitcast_fusion = (f32[16,1024]{1,0:T(8,128)S(1)}, f32[16,1024]{1,0:T(8,128)S(1)}, f32[16,1024]{1,0:T(8,128)S(1)}, f32[16,1024]{1,0:T(8,128)S(1)}, f32[16,1024]{1,0:T(8,128)}) fusion(f32[1024,16]{0,1:T(8,128)} %param.11, f32[1024,16]{0,1:T(8,128)} %param.12), kind=kLoop, calls=%fused_computation.13 | loop fusion | flops 81920 | bytes 458752 | tf_op jit(solution)/shard_map/neg | solution.py:186
  14.3 1.4 %divide_multiply_fusion.inter_ref = f32[16,8,1024]{2,1,0:T(8,128)} fusion(f32[8]{0:T(128)S(1)} %bitcast.57, f32[16,1024]{1,0:T(8,128)S(1)} %get-tuple-element.10, f32[16,1024]{1,0:T(8,128)S(1)} %bitcast_multiply_fusion), kind=kLoop, calls=%fused_computation.6 | loop fusion | flops 262144 | bytes 655392 | tf_op jit(solution)/shard_map/mul | solution.py:158
  15.6 1.6 %divide_multiply_fusion.1 = (f32[8,16,1024]{2,1,0:T(8,128)}, f32[8,1024]{1,0:T(8,128)}) fusion(f32[8]{0:T(128)S(1)} %bitcast.58, f32[16,1024]{1,0:T(8,128)S(1)} %get-tuple-element.10, f32[16,1024]{1,0:T(8,128)S(1)} %get-tuple-element.11, f32[16,1024]{1,0:T(8,128)S(1)} %get-tuple-element.12), kind=kLoop, calls=%fused_computation.8 | loop fusion | flops 516096 | bytes 753696 | tf_op jit(solution)/shard_map/mul | solution.py:156
  17.2 7.9 %collective-permute-done.halo_ref = bf16[3,144,1024]{2,1,0:T(8,128)(2,1)S(1)} collective-permute-done((bf16[3,144,1024]{2,1,0:T(8,128)(2,1)S(1)}, bf16[3,144,1024]{2,1,0:T(8,128)(2,1)S(1)}, u32[]{:S(2)}, u32[]{:S(2)}) %collective-permute-start) | collective-permute-done | bytes 884768 | tf_op jit(solution)/shard_map/ppermute | solution.py:19
  25.1 0.0 copy-start
  25.1 0.9 copy-done
  26.0 40.5 %shard_map.73.x_ref = bf16[2048,1024]{1,0:T(8,128)(2,1)} custom-call(bf16[3,2048,1024]{2,1,0:T(8,128)(2,1)} %bitcast.53, bf16[3,144,1024]{2,1,0:T(8,128)(2,1)} %copy-done, f32[3,7,1024]{2,1,0:T(8,128)} %bitcast.55, f32[64,256]{1,0:T(8,128)} %maximum_maximum_fusion.rows_ref, bf16[2048,2,1024]{2,1,0:T(2,128)(2,1)} %gate_ref.3), custom_call_target="tpu_custom_call" | custom-call | tf_op jit(solution)/shard_map/pallas_call | solution.py:272
  66.4 13.3 %shard_map.74 = f32[16,1024]{1,0:T(8,128)} custom-call(bf16[2048,1024]{1,0:T(8,128)(2,1)} %shard_map.73.x_ref, bf16[64,256]{1,0:T(8,128)(2,1)} %pad_maximum_fusion.2.mom_ref, f32[8,16,1024]{2,1,0:T(8,128)} %get-tuple-element.5.cs_ref, f32[16,1024]{1,0:T(8,128)} %get-tuple-element.13.l16_ref), custom_call_target="tpu_custom_call" | custom-call | tf_op jit(solution)/shard_map/pallas_call | solution.py:165
  79.8 15.2 %all-gather = f32[64,1024]{1,0:T(8,128)S(1)} all-gather(f32[16,1024]{1,0:T(8,128)} %shard_map.74), channel_id=2, replica_groups=mesh['groups'=2,'ctx'=4,'mp'=2,'sub'=2] {'ctx'}, dimensions={0}, use_global_device_ids=true | all-gather | bytes 327680 | tf_op jit(solution)/shard_map/all_gather | solution.py:180
  95.0 0.7 multiply_reduce_fusion.1.zin_ref
  95.7 32.9 %shard_map.75 = bf16[2048,1024]{1,0:T(8,128)(2,1)} custom-call(bf16[2048,1024]{1,0:T(8,128)(2,1)} %shard_map.73.x_ref, bf16[2048,2,1024]{2,1,0:T(2,128)(2,1)} %gate_ref.3, bf16[1024,256]{1,0:T(8,128)(2,1)} %pad_maximum_fusion.phi_ref, bf16[64,256]{1,0:T(8,128)(2,1)} %pad_maximum_fusion.2.mom_ref, bf16[128,192]{1,0:T(8,128)(2,1)} %pad_maximum_fusion.1.psi_ref, ...), custom_call_target="tpu_custom_call" | custom-call | tf_op jit(solution)/shard_map/pallas_call | solution.py:191
  (20 shorter events, 0.2 us)
Async XLA Ops:
  1.2 23.9 %collective-permute-start = (bf16[3,144,1024]{2,1,0:T(8,128)(2,1)S(1)}, bf16[3,144,1024]{2,1,0:T(8,128)(2,1)S(1)}, u32[]{:S(2)}, u32[]{:S(2)}) collective-permute-start(bf16[3,144,1024]{2,1,0:T(8,128)(2,1)S(1)} %slice.4), channel_id=1, source_target_pairs={{0,4},{4,8},{8,12},{1,5},{5,9},{9,13},{2,6},{6,10},{10,14},{3,7},{... | collective-permute-start | bytes 2654216 | tf_op jit(solution)/shard_map/ppermute | solution.py:19
  25.1 0.9 copy-start

commit v3 on v2

--- a/solution.py
+++ b/solution.py
@@ -113,7 +113,7 @@
     high, low = split_pair(jnp.concatenate(parts, 0))
     far = jnp.dot(psi_ref[...], jnp.concatenate([high, low, high], 0), preferred_element_type=jnp.float32)
     total = y + far + skip_ref[...] * xb.astype(jnp.float32)
-    o_ref[...] = (gate_ref[:, 0, :].astype(jnp.float32) * total).astype(o_ref.dtype)
+    o_ref[...] = (gate_ref[...].astype(jnp.float32) * total).astype(o_ref.dtype)
 
 
 def bases(rows):
@@ -193,7 +193,7 @@
         grid=grid,
         in_specs=[
             pl.BlockSpec((rows, lanes), lambda j, b: (b, j)),
-            pl.BlockSpec((rows, 2, lanes), lambda j, b: (b, 0, j)),
+            pl.BlockSpec((rows, lanes), lambda j, b: (b, j)),
             pl.BlockSpec((TERMS * rows, 2 * rows), lambda j, b: (0, 0)),
             pl.BlockSpec((subs_terms, 2 * rows), lambda j, b: (0, 0)),
             pl.BlockSpec((rows, 3 * subs_terms), lambda j, b: (0, 0)),
@@ -211,10 +211,10 @@
     )(lr_input, gate0, phi, mom, psi, ci, cs, inter, l16, incoming, lr_skip[None, :])
 
 
-HALO = 144
-
-
-def front_kernel(feat_ref, halo_ref, sf_ref, rows_ref, gate_ref, o_ref, ext_ref, prod_ref):
+RIM = 8
+
+
+def front_kernel(feat_ref, rim_ref, tail_ref, sf_ref, rows_ref, gate_ref, o_ref, ext_ref, prod_ref):
     count = feat_ref.shape[1]
     lanes = feat_ref.shape[2]
     groups = rows_ref.shape[0]
@@ -227,8 +227,9 @@
         for g in range(groups)
     ]
     for i in range(3):
-        ext_ref[i, 0:HALO, :] = halo_ref[i].astype(jnp.float32)
-        ext_ref[i, HALO : HALO + count, :] = feat_ref[i].astype(jnp.float32)
+        ext_ref[i, 0:RIM, :] = rim_ref[i].astype(jnp.float32)
+        ext_ref[i, RIM : RIM + count, :] = feat_ref[i].astype(jnp.float32)
+    prod_ref[0:taps, :] = tail_ref[...]
     taps_row = [[sf_ref[i, j : j + 1, :] for j in range(width)] for i in range(3)]
 
     def plane(i, e0):
@@ -238,23 +239,21 @@
         return total
 
     lane_group = lax.broadcasted_iota(jnp.int32, (taps, lanes), 1) // (lanes // groups)
-    for t0 in range(-taps, count, taps):
-        e0 = t0 + HALO
+    for t0 in range(0, count, taps):
+        e0 = t0 + RIM
         prod = (plane(1, e0) * plane(2, e0)).astype(jnp.bfloat16)
-        prod_ref[e0 : e0 + taps, :] = prod
-        if t0 < 0:
-            continue
-        window = prod_ref[e0 - taps : e0 + taps, :]
+        prod_ref[t0 + taps : t0 + 2 * taps, :] = prod
+        window = prod_ref[t0 : t0 + 2 * taps, :]
         mixed = None
         for g in range(groups):
             res = jnp.dot(toep[g], window, preferred_element_type=jnp.float32)
             mixed = res if mixed is None else jnp.where(lane_group == g, res, mixed)
         query = plane(0, e0)
-        gate = gate_ref[t0 : t0 + taps, 1, :].astype(jnp.float32)
+        gate = gate_ref[t0 : t0 + taps, :].astype(jnp.float32)
         o_ref[t0 : t0 + taps, :] = (gate * query * mixed).astype(o_ref.dtype)
 
 
-def front(planes, halo, short_filter, mr_filter, gates):
+def front(planes, rim, tail, short_filter, mr_filter, gate1):
     _, count, chans = planes.shape
     groups, taps = mr_filter.shape
     lanes = 128
@@ -274,27 +273,34 @@
         grid=(chans // lanes,),
         in_specs=[
             pl.BlockSpec((3, count, lanes), lambda j: (0, 0, j)),
-            pl.BlockSpec((3, HALO, lanes), lambda j: (0, 0, j)),
+            pl.BlockSpec((3, RIM, lanes), lambda j: (0, 0, j)),
+            pl.BlockSpec((taps, lanes), lambda j: (0, j)),
             pl.BlockSpec((3, width, lanes), lambda j: (0, 0, j)),
             pl.BlockSpec((per_tile, 2 * taps), lambda j: (j, 0)),
-            pl.BlockSpec((count, 2, lanes), lambda j: (0, 0, j)),
+            pl.BlockSpec((count, lanes), lambda j: (0, j)),
         ],
         out_specs=pl.BlockSpec((count, lanes), lambda j: (0, j)),
         out_shape=jax.ShapeDtypeStruct((count, chans), jnp.bfloat16),
         scratch_shapes=[
-            pltpu.VMEM((3, HALO + count, lanes), jnp.float32),
-            pltpu.VMEM((HALO + count, lanes), jnp.bfloat16),
+            pltpu.VMEM((3, RIM + count, lanes), jnp.float32),
+            pltpu.VMEM((taps + count, lanes), jnp.bfloat16),
         ],
         compiler_params=pltpu.CompilerParams(dimension_semantics=("arbitrary",)),
-    )(planes, halo, sf, template, gates)
+    )(planes, rim, tail, sf, template, gate1)
 
 
 def per_device(features, short_filter, mr_filter, lr_gates, lr_rate, lr_residue, lr_skip):
     count = features.shape[0]
+    taps = mr_filter.shape[1]
+    width = short_filter.shape[0]
     planes = features.transpose(1, 0, 2)
-    halo = passed_along(planes[:, count - HALO :], "ctx", 1)
-    lr_input = front(planes, halo, short_filter, mr_filter, lr_gates)
-    return long_conv_out(lr_input, lr_gates, lr_rate, lr_residue, lr_skip)
+    recent = planes[1:, count - taps - (width - 1) :].astype(jnp.float32)
+    key = featurize(recent[0], short_filter[:, 1])
+    value = featurize(recent[1], short_filter[:, 2])
+    tail = passed_along((key * value).astype(jnp.bfloat16), "ctx", 1)
+    rim = passed_along(planes[:, count - RIM :], "ctx", 1)
+    lr_input = front(planes, rim, tail, short_filter, mr_filter, lr_gates[:, 1, :])
+    return long_conv_out(lr_input, lr_gates[:, 0, :], lr_rate, lr_residue, lr_skip)
 
 
 def solution(mesh):

time: 129 us -> 137 us (1.062)
  local copies, waits for them, and re-layouts: 3.28 us -> 27 us
  Pallas kernels: 86.7 us -> 74.4 us
  waiting for transfers between devices: 7.87 us -> 0.01 us
  starting transfers between devices: 5.01 us -> 8.44 us
    slice x1 -> x3, local copies, waits for them, and re-layouts: 1.22 us -> 15.1 us  [the longest x1 13.1 us: per_device(): lr_gates[:, 0, :]]
    unnamed x2 -> x16, local copies, waits for them, and re-layouts: 0.91 us -> 11.5 us
    pallas_call x1, Pallas kernels: 40.5 us -> 30.1 us  [front(): pl.pallas_call(front_kernel, grid=(chans // lanes,), in_specs=[pl.BlockSp...]
    ppermute x1 -> x2, waiting for transfers between devices: 7.87 us -> 0.01 us  [passed_along(): return lax.ppermute(shard, axis, pairs)]
    ppermute x1 -> x2, starting transfers between devices: 5.01 us -> 8.44 us  [passed_along(): return lax.ppermute(shard, axis, pairs)]
    convert_element_type x0 -> x2, other arithmetic: none -> 2.84 us  [the longest x1 1.96 us: per_device(): recent = planes[1:, count - taps - (width - 1):].astype(jnp.float32)]
    pallas_call x1, Pallas kernels: 32.9 us -> 30.9 us  [long_conv_out(): pl.pallas_call(main_kernel, grid=grid, in_specs=[pl.BlockSpec((rows, lane...]
  transfers between devices with their start and end apart: 1 -> 2, of which waited for: 1 -> 0; matrix products, arithmetic and copies ran while one was open for 8% -> 24% of each run, Pallas kernels for 0% -> 0%
where the time goes in v3:
time: 137 us; the launch traced here: 136 us
  Pallas kernels  74.4 us (54%)
  local copies, waits for them, and re-layouts  27 us (20%)
  blocking collectives  14.6 us (11%)
  other arithmetic  11.5 us (8%)
  starting transfers between devices  8.44 us (6%)
    pallas_call x1, Pallas kernels, long_conv_out(): pl.pallas_call(main_kernel, grid=grid, in_specs=[pl.BlockSpec((rows, lane...  30.9 us
    pallas_call x1, Pallas kernels, front(): pl.pallas_call(front_kernel, grid=(chans // lanes,), in_specs=[pl.BlockSp...  30.1 us
    all_gather x1, blocking collectives, long_conv_out(): states = lax.all_gather(final, 'ctx')  14.6 us
    pallas_call x1, Pallas kernels, long_conv_out(): pl.pallas_call(state_kernel, grid=grid, in_specs=[pl.BlockSpec((rows, lan...  13.3 us
    slice x1, local copies, waits for them, and re-layouts, per_device(): lr_gates[:, 0, :]  13.1 us
    unnamed x16, local copies, waits for them, and re-layouts  11.5 us
    ppermute x2, starting transfers between devices, passed_along(): return lax.ppermute(shard, axis, pairs)  8.44 us
  transfers between devices with their start and end apart: 2, of which 0 were waited for; matrix products, arithmetic and copies ran while one was open for 24% of the time, Pallas kernels for 0%

profile of v3, /device:TPU:0, one launch (start us, length us, event | category | flops | bytes accessed | tf_op | source)
XLA Modules:
  0.0 136.1 jit_solution(9479798603034475565)
XLA Ops:
  0.0 0.0 copy-start.3
  0.0 0.0 copy-start.4
  0.0 0.0 copy-start
  0.0 1.2 fusion.37
  1.2 2.0 %slice_convert_fusion = f32[2,134,1024]{2,1,0:T(8,128)S(1)} fusion(bf16[3,2048,1024]{2,1,0:T(8,128)(2,1)} %bitcast.184), kind=kLoop, calls=%fused_computation.2 | loop fusion | flops 274432 | bytes 1646592 | tf_op jit(solution)/shard_map/convert_element_type | solution.py:297
  3.2 0.9 fusion.3
  4.1 5.0 %collective-permute-start.1 = (bf16[128,1024]{1,0:T(8,128)(2,1)S(1)}, bf16[128,1024]{1,0:T(8,128)(2,1)S(1)}, u32[]{:S(2)}, u32[]{:S(2)}) collective-permute-start(bf16[128,1024]{1,0:T(8,128)(2,1)S(1)} %fusion.3), channel_id=1, source_target_pairs={{0,4},{4,8},{8,12},{1,5},{5,9},{9,13},{2,6},{6,10},{10,14},{3,7},{... | collective-permute-start | bytes 786440 | tf_op jit(solution)/shard_map/ppermute | solution.py:19
  9.1 0.8 slice.230
  9.9 3.5 %collective-permute-start = (bf16[3,8,1024]{2,1,0:T(8,128)(2,1)S(1)}, bf16[3,8,1024]{2,1,0:T(8,128)(2,1)S(1)}, u32[]{:S(2)}, u32[]{:S(2)}) collective-permute-start(bf16[3,8,1024]{2,1,0:T(8,128)(2,1)S(1)} %slice.230), channel_id=1, source_target_pairs={{0,4},{4,8},{8,12},{1,5},{5,9},{9,13},{2,6},{6,10},{10,14},{3,7},{... | collective-permute-start | bytes 147464 | tf_op jit(solution)/shard_map/ppermute | solution.py:19
  13.5 0.1 fusion.32
  13.7 0.0 copy-done.3
  13.7 0.0 copy-done.4
  13.7 0.7 negate_bitcast_fusion
  14.4 0.0 copy-done
  14.4 0.0 copy-start.6
  14.4 13.1 %fusion.36 = (bf16[2048,1,1024]{2,1,0:T(2,128)(2,1)}, bf16[2048,1,1024]{2,1,0:T(2,128)(2,1)}) fusion(bf16[2048,2,1024]{2,1,0:T(2,128)(2,1)S(1)} %copy-done), kind=kLoop, calls=%fused_computation.91 | loop fusion | bytes 16777216 | tf_op jit(solution)/shard_map/slice | solution.py:303
  27.5 0.0 copy-done.6
  27.5 0.1 rev.3
  27.6 0.1 pad.9.clone
  27.7 0.1 copy.18
  27.8 0.1 copy.17
  27.9 0.7 pad_maximum_fusion.1.psi_ref
  28.6 0.2 reduce-window.8
  28.8 1.4 divide_multiply_fusion.inter_ref
  30.1 1.6 %divide_multiply_fusion.1 = (f32[8,16,1024]{2,1,0:T(8,128)}, f32[8,1024]{1,0:T(8,128)}) fusion(f32[8]{0:T(128)S(1)} %bitcast.205, f32[16,1024]{1,0:T(8,128)S(1)} %get-tuple-element.26, f32[16,1024]{1,0:T(8,128)S(1)} %get-tuple-element.27, f32[16,1024]{1,0:T(8,128)S(1)} %get-tuple-element.28), kind=kLoop, calls=%fused_computation.53 | loop fusion | flops 516096 | bytes 753696 | tf_op jit(solution)/shard_map/mul | solution.py:156
  31.7 0.6 pad_maximum_fusion.2.mom_ref
  32.3 0.0 copy-start.1
  32.3 0.7 maximum_maximum_fusion.rows_ref
  33.0 1.0 fusion.30
  34.0 0.9 pad_maximum_fusion.phi_ref
  34.9 7.1 %copy.25 = bf16[2048,1,1024]{2,0,1:T(8,128)(2,1)} copy(bf16[2048,1,1024]{2,1,0:T(2,128)(2,1)} %get-tuple-element.6) | data formatting | bytes 8388608
  42.0 0.0 copy-done.1
  42.0 3.6 %copy.24 = bf16[2048,1,1024]{2,0,1:T(8,128)(2,1)} copy(bf16[2048,1,1024]{2,1,0:T(2,128)(2,1)S(1)} %copy-done.1) | data formatting | bytes 8388608
  45.7 0.0 collective-permute-done.rim_ref
  45.7 0.0 copy-start.5
  45.7 0.0 collective-permute-done.1.tail_ref
  45.7 0.0 copy-start.2
  45.7 0.6 copy-done.5
  46.3 0.1 copy-done.2
  46.4 30.1 %shard_map.73.x_ref = bf16[2048,1024]{1,0:T(8,128)(2,1)} custom-call(bf16[3,2048,1024]{2,1,0:T(8,128)(2,1)} %bitcast.186, bf16[3,8,1024]{2,1,0:T(8,128)(2,1)} %copy-done.5, bf16[128,1024]{1,0:T(8,128)(2,1)} %copy-done.2, f32[3,7,1024]{2,1,0:T(8,128)} %bitcast.188, f32[64,256]{1,0:T(8,128)} %maximum_maximum_fusion.rows_ref, bf16[2048,1024]{1,0:T(8,128)(2,1)} %bitcast.183), custom_call_target="tpu_custom_call" | custom-call | tf_op jit(solution)/shard_map/pallas_call | solution.py:271
  76.5 13.3 %shard_map.74 = f32[16,1024]{1,0:T(8,128)} custom-call(bf16[2048,1024]{1,0:T(8,128)(2,1)} %shard_map.73.x_ref, bf16[64,256]{1,0:T(8,128)(2,1)} %pad_maximum_fusion.2.mom_ref, f32[8,16,1024]{2,1,0:T(8,128)} %get-tuple-element.7.cs_ref, f32[16,1024]{1,0:T(8,128)} %get-tuple-element.29.l16_ref), custom_call_target="tpu_custom_call" | custom-call | tf_op jit(solution)/shard_map/pallas_call | solution.py:165
  89.8 14.6 %all-gather = f32[64,1024]{1,0:T(8,128)S(1)} all-gather(f32[16,1024]{1,0:T(8,128)} %shard_map.74), channel_id=2, replica_groups=mesh['groups'=2,'ctx'=4,'mp'=2,'sub'=2] {'ctx'}, dimensions={0}, use_global_device_ids=true | all-gather | bytes 327680 | tf_op jit(solution)/shard_map/all_gather | solution.py:180
  104.5 0.7 multiply_reduce_fusion.1.zin_ref
  105.2 30.9 %shard_map.75 = bf16[2048,1024]{1,0:T(8,128)(2,1)} custom-call(bf16[2048,1024]{1,0:T(8,128)(2,1)} %shard_map.73.x_ref, bf16[2048,1024]{1,0:T(8,128)(2,1)} %bitcast.182, bf16[1024,256]{1,0:T(8,128)(2,1)} %pad_maximum_fusion.phi_ref, bf16[64,256]{1,0:T(8,128)(2,1)} %pad_maximum_fusion.2.mom_ref, bf16[128,192]{1,0:T(8,128)(2,1)} %pad_maximum_fusion.1.psi_ref, ...), custom_call_target="tpu_custom_call" | custom-call | tf_op jit(solution)/shard_map/pallas_call | solution.py:191
  (21 shorter events, 0.2 us)
Async XLA Ops:
  0.0 13.7 %copy-start.3 = (f32[1024,16]{0,1:T(8,128)S(1)}, f32[1024,16]{0,1:T(8,128)}, u32[]{:S(2)}) copy-start(f32[1024,16]{0,1:T(8,128)} %param.11) | copy-start | bytes 196612
  0.0 13.7 %copy-start.4 = (f32[1024,16]{0,1:T(8,128)S(1)}, f32[1024,16]{0,1:T(8,128)}, u32[]{:S(2)}) copy-start(f32[1024,16]{0,1:T(8,128)} %param.12) | copy-start | bytes 196612
  0.0 14.4 %copy-start = (bf16[2048,2,1024]{2,1,0:T(2,128)(2,1)S(1)}, bf16[2048,2,1024]{2,1,0:T(2,128)(2,1)}, u32[]{:S(2)}) copy-start(bf16[2048,2,1024]{2,1,0:T(2,128)(2,1)} %param.10) | copy-start | bytes 25165828
  4.1 41.6 %collective-permute-start.1 = (bf16[128,1024]{1,0:T(8,128)(2,1)S(1)}, bf16[128,1024]{1,0:T(8,128)(2,1)S(1)}, u32[]{:S(2)}, u32[]{:S(2)}) collective-permute-start(bf16[128,1024]{1,0:T(8,128)(2,1)S(1)} %fusion.3), channel_id=1, source_target_pairs={{0,4},{4,8},{8,12},{1,5},{5,9},{9,13},{2,6},{6,10},{10,14},{3,7},{... | collective-permute-start | bytes 786440 | tf_op jit(solution)/shard_map/ppermute | solution.py:19
  9.9 35.8 %collective-permute-start = (bf16[3,8,1024]{2,1,0:T(8,128)(2,1)S(1)}, bf16[3,8,1024]{2,1,0:T(8,128)(2,1)S(1)}, u32[]{:S(2)}, u32[]{:S(2)}) collective-permute-start(bf16[3,8,1024]{2,1,0:T(8,128)(2,1)S(1)} %slice.230), channel_id=1, source_target_pairs={{0,4},{4,8},{8,12},{1,5},{5,9},{9,13},{2,6},{6,10},{10,14},{3,7},{... | collective-permute-start | bytes 147464 | tf_op jit(solution)/shard_map/ppermute | solution.py:19
  14.4 13.1 %copy-start.6 = (bf16[64,128]{1,0:T(8,128)(2,1)S(1)}, bf16[64,128]{1,0:T(8,128)(2,1)}, u32[]{:S(2)}) copy-start(bf16[64,128]{1,0:T(8,128)(2,1)} %param.9) | copy-start | bytes 49156
  32.3 9.7 %copy-start.1 = (bf16[2048,1,1024]{2,1,0:T(2,128)(2,1)S(1)}, bf16[2048,1,1024]{2,1,0:T(2,128)(2,1)}, u32[]{:S(2)}) copy-start(bf16[2048,1,1024]{2,1,0:T(2,128)(2,1)} %get-tuple-element.5) | copy-start | bytes 12582916
  45.7 0.6 copy-start.5
  45.7 0.7 copy-start.2

commit v4 on v2

--- a/solution.py
+++ b/solution.py
@@ -113,7 +113,7 @@
     high, low = split_pair(jnp.concatenate(parts, 0))
     far = jnp.dot(psi_ref[...], jnp.concatenate([high, low, high], 0), preferred_element_type=jnp.float32)
     total = y + far + skip_ref[...] * xb.astype(jnp.float32)
-    o_ref[...] = (gate_ref[:, 0, :].astype(jnp.float32) * total).astype(o_ref.dtype)
+    o_ref[...] = (gate_ref[...].astype(jnp.float32) * total).astype(o_ref.dtype)
 
 
 def bases(rows):
@@ -177,23 +177,18 @@
         compiler_params=params,
     )(lr_input, mom, cs, l16)
 
-    states = lax.all_gather(final, "ctx")
-    devices = states.shape[0]
-    me = lax.axis_index("ctx")
-    gap = (me - 1 - jnp.arange(devices)).astype(jnp.float32)
-    carry = jnp.where(
-        (gap >= 0)[:, None, None],
-        jnp.exp(-rate[None] * (jnp.maximum(gap, 0.0) * count)[:, None, None]),
-        0.0,
-    )
-    incoming = jnp.sum(carry * states, axis=0)
+    devices = lax.axis_size("ctx")
+    incoming = jnp.zeros_like(final)
+    for shift in range(1, devices):
+        earlier = passed_along(final, "ctx", shift)
+        incoming = incoming + jnp.exp(-rate * float((shift - 1) * count)) * earlier
 
     return pl.pallas_call(
         main_kernel,
         grid=grid,
         in_specs=[
             pl.BlockSpec((rows, lanes), lambda j, b: (b, j)),
-            pl.BlockSpec((rows, 2, lanes), lambda j, b: (b, 0, j)),
+            pl.BlockSpec((rows, lanes), lambda j, b: (b, j)),
             pl.BlockSpec((TERMS * rows, 2 * rows), lambda j, b: (0, 0)),
             pl.BlockSpec((subs_terms, 2 * rows), lambda j, b: (0, 0)),
             pl.BlockSpec((rows, 3 * subs_terms), lambda j, b: (0, 0)),
@@ -250,11 +245,11 @@
             res = jnp.dot(toep[g], window, preferred_element_type=jnp.float32)
             mixed = res if mixed is None else jnp.where(lane_group == g, res, mixed)
         query = plane(0, e0)
-        gate = gate_ref[t0 : t0 + taps, 1, :].astype(jnp.float32)
+        gate = gate_ref[t0 : t0 + taps, :].astype(jnp.float32)
         o_ref[t0 : t0 + taps, :] = (gate * query * mixed).astype(o_ref.dtype)
 
 
-def front(planes, halo, short_filter, mr_filter, gates):
+def front(planes, halo, short_filter, mr_filter, gate1):
     _, count, chans = planes.shape
     groups, taps = mr_filter.shape
     lanes = 128
@@ -277,7 +272,7 @@
             pl.BlockSpec((3, HALO, lanes), lambda j: (0, 0, j)),
             pl.BlockSpec((3, width, lanes), lambda j: (0, 0, j)),
             pl.BlockSpec((per_tile, 2 * taps), lambda j: (j, 0)),
-            pl.BlockSpec((count, 2, lanes), lambda j: (0, 0, j)),
+            pl.BlockSpec((count, lanes), lambda j: (0, j)),
         ],
         out_specs=pl.BlockSpec((count, lanes), lambda j: (0, j)),
         out_shape=jax.ShapeDtypeStruct((count, chans), jnp.bfloat16),
@@ -286,15 +281,16 @@
             pltpu.VMEM((HALO + count, lanes), jnp.bfloat16),
         ],
         compiler_params=pltpu.CompilerParams(dimension_semantics=("arbitrary",)),
-    )(planes, halo, sf, template, gates)
+    )(planes, halo, sf, template, gate1)
 
 
 def per_device(features, short_filter, mr_filter, lr_gates, lr_rate, lr_residue, lr_skip):
     count = features.shape[0]
     planes = features.transpose(1, 0, 2)
     halo = passed_along(planes[:, count - HALO :], "ctx", 1)
-    lr_input = front(planes, halo, short_filter, mr_filter, lr_gates)
-    return long_conv_out(lr_input, lr_gates, lr_rate, lr_residue, lr_skip)
+    gates = lr_gates.transpose(1, 0, 2)
+    lr_input = front(planes, halo, short_filter, mr_filter, gates[1])
+    return long_conv_out(lr_input, gates[0], lr_rate, lr_residue, lr_skip)
 
 
 def solution(mesh):

time: 129 us -> 118 us (0.915)
  local copies, waits for them, and re-layouts: 3.28 us -> 18.6 us
  blocking collectives: 15.2 us -> 0 us
  Pallas kernels: 86.7 us -> 74.7 us
  starting transfers between devices: 5.01 us -> 12.6 us
  waiting for transfers between devices: 7.87 us -> 1.48 us
    all_gather x1 -> x0, blocking collectives: 15.2 us -> none  [long_conv_out(): states = lax.all_gather(final, 'ctx')]
    pallas_call x1, Pallas kernels: 40.5 us -> 30.4 us  [front(): pl.pallas_call(front_kernel, grid=(chans // lanes,), in_specs=[pl.BlockSp...]
    unnamed x2 -> x7, local copies, waits for them, and re-layouts: 0.91 us -> 10.2 us
    ppermute x1 -> x4, starting transfers between devices: 5.01 us -> 12.6 us  [passed_along(): return lax.ppermute(shard, axis, pairs)]
    ppermute x1 -> x4, waiting for transfers between devices: 7.87 us -> 1.48 us  [passed_along(): return lax.ppermute(shard, axis, pairs)]
    squeeze x0 -> x1, local copies, waits for them, and re-layouts: none -> 6.02 us  [per_device(): return long_conv_out(lr_input, gates[0], lr_rate, lr_residue, lr_skip)]
    pallas_call x1, Pallas kernels: 32.9 us -> 30.9 us  [long_conv_out(): pl.pallas_call(main_kernel, grid=grid, in_specs=[pl.BlockSpec((rows, lane...]
    exp x0 -> x1, other arithmetic: none -> 1.53 us  [long_conv_out(): l16 = jnp.exp(-float(SUB) * rate)]
  transfers between devices with their start and end apart: 1 -> 4, of which waited for: 1 -> 2; matrix products, arithmetic and copies ran while one was open for 8% -> 20% of each run, Pallas kernels for 0% -> 0%
where the time goes in v4:
time: 118 us; the launch traced here: 117 us
  Pallas kernels  74.7 us (63%)
  local copies, waits for them, and re-layouts  18.6 us (16%)
  starting transfers between devices  12.6 us (11%)
  other arithmetic  9.49 us (8%)
  waiting for transfers between devices  1.48 us (1%)
    pallas_call x1, Pallas kernels, long_conv_out(): pl.pallas_call(main_kernel, grid=grid, in_specs=[pl.BlockSpec((rows, lane...  30.9 us
    pallas_call x1, Pallas kernels, front(): pl.pallas_call(front_kernel, grid=(chans // lanes,), in_specs=[pl.BlockSp...  30.4 us
    pallas_call x1, Pallas kernels, long_conv_out(): pl.pallas_call(state_kernel, grid=grid, in_specs=[pl.BlockSpec((rows, lan...  13.4 us
    ppermute x4, starting transfers between devices, passed_along(): return lax.ppermute(shard, axis, pairs)  12.6 us
    unnamed x7, local copies, waits for them, and re-layouts  10.2 us
    squeeze x1, local copies, waits for them, and re-layouts, per_device(): return long_conv_out(lr_input, gates[0], lr_rate, lr_residue, lr_skip)  6.02 us
  transfers between devices with their start and end apart: 4, of which 2 were waited for; matrix products, arithmetic and copies ran while one was open for 20% of the time, Pallas kernels for 0%

profile of v4, /device:TPU:0, one launch (start us, length us, event | category | flops | bytes accessed | tf_op | source)
XLA Modules:
  0.0 117.0 jit_solution(5838266082640106307)
XLA Ops:
  0.0 1.2 %slice.12 = bf16[3,144,1024]{2,1,0:T(8,128)(2,1)S(1)} slice(bf16[3,2048,1024]{2,1,0:T(8,128)(2,1)} %bitcast.71), slice={[0:3], [1904:2048], [0:1024]} | slice | bytes 1769472 | tf_op jit(solution)/shard_map/slice | solution.py:290
  1.2 5.0 %collective-permute-start = (bf16[3,144,1024]{2,1,0:T(8,128)(2,1)S(1)}, bf16[3,144,1024]{2,1,0:T(8,128)(2,1)S(1)}, u32[]{:S(2)}, u32[]{:S(2)}) collective-permute-start(bf16[3,144,1024]{2,1,0:T(8,128)(2,1)S(1)} %slice.12), channel_id=1, source_target_pairs={{0,4},{4,8},{8,12},{1,5},{5,9},{9,13},{2,6},{6,10},{10,14},{3,7},{... | collective-permute-start | bytes 2654216 | tf_op jit(solution)/shard_map/ppermute | solution.py:19
  6.4 0.1 fusion.6
  6.6 0.8 rev.3
  7.4 0.1 pad.9.clone
  7.5 0.1 copy.15
  7.6 0.1 copy.14
  7.7 1.5 %exponential_bitcast_fusion = (f32[16,1024]{1,0:T(8,128)}, f32[16,1024]{1,0:T(8,128)S(1)}, f32[16,1024]{1,0:T(8,128)S(1)}, f32[16,1024]{1,0:T(8,128)S(1)}) fusion(f32[1024,16]{0,1:T(8,128)} %param.11, f32[1024,16]{0,1:T(8,128)} %param.12), kind=kLoop, calls=%fused_computation.20 | loop fusion | flops 65536 | bytes 393216 | tf_op jit(solution)/shard_map/exp | solution.py:159
  9.2 0.2 reduce-window.8
  9.4 0.7 maximum_maximum_fusion.rows_ref
  10.1 1.0 fusion.2
  11.2 1.6 %divide_multiply_fusion.1 = (f32[8,16,1024]{2,1,0:T(8,128)}, f32[8,1024]{1,0:T(8,128)}) fusion(f32[8]{0:T(128)S(1)} %bitcast.75, f32[16,1024]{1,0:T(8,128)S(1)} %get-tuple-element.14, f32[16,1024]{1,0:T(8,128)S(1)} %get-tuple-element.15, f32[16,1024]{1,0:T(8,128)S(1)} %get-tuple-element.16), kind=kLoop, calls=%fused_computation.11 | loop fusion | flops 516096 | bytes 753696 | tf_op jit(solution)/shard_map/mul | solution.py:156
  12.7 0.9 pad_maximum_fusion.phi_ref
  13.6 9.3 %copy.18 = bf16[2048,2,1024]{2,0,1:T(8,128)(2,1)} copy(bf16[2048,2,1024]{2,1,0:T(2,128)(2,1)} %param.10) | data formatting | bytes 16777216 | tf_op args[3]
  22.9 0.6 pad_maximum_fusion.2.mom_ref
  23.5 6.0 %slice_bitcast_fusion = (bf16[2048,1024]{1,0:T(8,128)(2,1)}, bf16[2048,1024]{1,0:T(8,128)(2,1)}) fusion(bf16[2,2048,1024]{2,1,0:T(8,128)(2,1)} %bitcast.70), kind=kLoop, calls=%fused_computation.1 | loop fusion | bytes 16777216 | tf_op jit(solution)/shard_map/squeeze | solution.py:293
  29.5 0.0 collective-permute-done.halo_ref
  29.5 0.0 copy-start
  29.5 0.9 copy-done
  30.5 30.4 %shard_map.73.x_ref = bf16[2048,1024]{1,0:T(8,128)(2,1)} custom-call(bf16[3,2048,1024]{2,1,0:T(8,128)(2,1)} %bitcast.72, bf16[3,144,1024]{2,1,0:T(8,128)(2,1)} %copy-done, f32[3,7,1024]{2,1,0:T(8,128)} %bitcast.73, f32[64,256]{1,0:T(8,128)} %maximum_maximum_fusion.rows_ref, bf16[2048,1024]{1,0:T(8,128)(2,1)} %get-tuple-element.6.gate_ref), custom_call_target="tpu_custom_call" | custom-call | tf_op jit(solution)/shard_map/pallas_call | solution.py:267
  60.8 0.0 copy-start.1
  60.8 0.0 copy-start.2
  60.8 13.4 %shard_map.74 = f32[16,1024]{1,0:T(8,128)} custom-call(bf16[2048,1024]{1,0:T(8,128)(2,1)} %shard_map.73.x_ref, bf16[64,256]{1,0:T(8,128)(2,1)} %pad_maximum_fusion.2.mom_ref, f32[8,16,1024]{2,1,0:T(8,128)} %get-tuple-element.7.cs_ref, f32[16,1024]{1,0:T(8,128)} %get-tuple-element.13.l16_ref), custom_call_target="tpu_custom_call" | custom-call | tf_op jit(solution)/shard_map/pallas_call | solution.py:165
  74.2 3.4 %collective-permute-start.1 = (f32[16,1024]{1,0:T(8,128)}, f32[16,1024]{1,0:T(8,128)S(1)}, u32[]{:S(2)}, u32[]{:S(2)}) collective-permute-start(f32[16,1024]{1,0:T(8,128)} %shard_map.74), channel_id=1, source_target_pairs={{0,4},{4,8},{8,12},{1,5},{5,9},{9,13},{2,6},{6,10},{10,14},{3,7},{... | collective-permute-start | bytes 196616 | tf_op jit(solution)/shard_map/ppermute | solution.py:19
  77.6 2.9 %collective-permute-start.2 = (f32[16,1024]{1,0:T(8,128)}, f32[16,1024]{1,0:T(8,128)S(1)}, u32[]{:S(2)}, u32[]{:S(2)}) collective-permute-start(f32[16,1024]{1,0:T(8,128)} %shard_map.74), channel_id=1, source_target_pairs={{0,8},{4,12},{1,9},{5,13},{2,10},{6,14},{3,11},{7,15},{16,24},{20,... | collective-permute-start | bytes 196616 | tf_op jit(solution)/shard_map/ppermute | solution.py:19
  80.6 1.3 %collective-permute-start.3 = (f32[16,1024]{1,0:T(8,128)}, f32[16,1024]{1,0:T(8,128)S(1)}, u32[]{:S(2)}, u32[]{:S(2)}) collective-permute-start(f32[16,1024]{1,0:T(8,128)} %shard_map.74), channel_id=1, source_target_pairs={{0,12},{1,13},{2,14},{3,15},{16,28},{17,29},{18,30},{19,31}} | collective-permute-start | bytes 196616 | tf_op jit(solution)/shard_map/ppermute | solution.py:19
  81.9 0.7 pad_maximum_fusion.1.psi_ref
  82.6 0.0 collective-permute-done.1
  82.6 0.7 collective-permute-done.2
  83.2 0.8 collective-permute-done.3
  84.1 0.0 copy-done.1
  84.1 0.0 copy-done.2
  84.1 0.7 fusion.4
  84.8 1.4 %divide_multiply_fusion.inter_ref = f32[16,8,1024]{2,1,0:T(8,128)} fusion(f32[8]{0:T(128)S(1)} %bitcast.76, f32[16,1024]{1,0:T(8,128)S(1)} %get-tuple-element.14, f32[16,1024]{1,0:T(8,128)S(1)} %get-tuple-element.12), kind=kLoop, calls=%fused_computation.9 | loop fusion | flops 262144 | bytes 655392 | tf_op jit(solution)/shard_map/mul | solution.py:158
  86.1 30.9 %shard_map.75 = bf16[2048,1024]{1,0:T(8,128)(2,1)} custom-call(bf16[2048,1024]{1,0:T(8,128)(2,1)} %shard_map.73.x_ref, bf16[2048,1024]{1,0:T(8,128)(2,1)} %get-tuple-element.5.gate_ref, bf16[1024,256]{1,0:T(8,128)(2,1)} %pad_maximum_fusion.phi_ref, bf16[64,256]{1,0:T(8,128)(2,1)} %pad_maximum_fusion.2.mom_ref, bf16[128,192]{1,0:T(8,128)(2,1)} %pad_maximum_fusion.1.psi_ref, ...), custom_call_target="tpu_custom_call" | custom-call | tf_op jit(solution)/shard_map/pallas_call | solution.py:186
  (18 shorter events, 0.2 us)
Async XLA Ops:
  1.2 28.3 %collective-permute-start = (bf16[3,144,1024]{2,1,0:T(8,128)(2,1)S(1)}, bf16[3,144,1024]{2,1,0:T(8,128)(2,1)S(1)}, u32[]{:S(2)}, u32[]{:S(2)}) collective-permute-start(bf16[3,144,1024]{2,1,0:T(8,128)(2,1)S(1)} %slice.12), channel_id=1, source_target_pairs={{0,4},{4,8},{8,12},{1,5},{5,9},{9,13},{2,6},{6,10},{10,14},{3,7},{... | collective-permute-start | bytes 2654216 | tf_op jit(solution)/shard_map/ppermute | solution.py:19
  29.5 0.9 copy-start
  60.8 23.2 %copy-start.1 = (f32[1024,16]{0,1:T(8,128)S(1)}, f32[1024,16]{0,1:T(8,128)}, u32[]{:S(2)}) copy-start(f32[1024,16]{0,1:T(8,128)} %param.11) | copy-start | bytes 196612
  60.8 23.2 %copy-start.2 = (f32[1024,16]{0,1:T(8,128)S(1)}, f32[1024,16]{0,1:T(8,128)}, u32[]{:S(2)}) copy-start(f32[1024,16]{0,1:T(8,128)} %param.12) | copy-start | bytes 196612
  74.2 8.4 %collective-permute-start.1 = (f32[16,1024]{1,0:T(8,128)}, f32[16,1024]{1,0:T(8,128)S(1)}, u32[]{:S(2)}, u32[]{:S(2)}) collective-permute-start(f32[16,1024]{1,0:T(8,128)} %shard_map.74), channel_id=1, source_target_pairs={{0,4},{4,8},{8,12},{1,5},{5,9},{9,13},{2,6},{6,10},{10,14},{3,7},{... | collective-permute-start | bytes 196616 | tf_op jit(solution)/shard_map/ppermute | solution.py:19
  77.6 5.6 %collective-permute-start.2 = (f32[16,1024]{1,0:T(8,128)}, f32[16,1024]{1,0:T(8,128)S(1)}, u32[]{:S(2)}, u32[]{:S(2)}) collective-permute-start(f32[16,1024]{1,0:T(8,128)} %shard_map.74), channel_id=1, source_target_pairs={{0,8},{4,12},{1,9},{5,13},{2,10},{6,14},{3,11},{7,15},{16,24},{20,... | collective-permute-start | bytes 196616 | tf_op jit(solution)/shard_map/ppermute | solution.py:19
  80.6 3.5 %collective-permute-start.3 = (f32[16,1024]{1,0:T(8,128)}, f32[16,1024]{1,0:T(8,128)S(1)}, u32[]{:S(2)}, u32[]{:S(2)}) collective-permute-start(f32[16,1024]{1,0:T(8,128)} %shard_map.74), channel_id=1, source_target_pairs={{0,12},{1,13},{2,14},{3,15},{16,28},{17,29},{18,30},{19,31}} | collective-permute-start | bytes 196616 | tf_op jit(solution)/shard_map/ppermute | solution.py:19

commit v5 on v4

--- a/solution.py
+++ b/solution.py
@@ -1,6 +1,7 @@
 import functools
 
 import jax
+import numpy as np
 import jax.numpy as jnp
 from jax import lax
 from jax.experimental import pallas as pl
@@ -58,20 +59,29 @@
     return high, low
 
 
+def tree_sum(values):
+    while len(values) > 1:
+        values = [values[i] + values[i + 1] if i + 1 < len(values) else values[i] for i in range(0, len(values), 2)]
+    return values[0]
+
+
 def carry_subblocks(moments, z, cs_ref, l16, inter_ref=None):
+    terms = cs_ref.shape[0]
+    subs = moments.shape[0] // terms
+    coefs = [cs_ref[n] for n in range(terms)]
+    accs = [
+        tree_sum([coefs[n] * moments[sb * terms + n : sb * terms + n + 1] for n in range(terms)])
+        for sb in range(subs)
+    ]
+    zs = []
+    for sb in range(subs):
+        zs.append(z)
+        z = l16 * z + accs[sb]
     parts = []
-    terms = cs_ref.shape[0]
-    modes = z.shape[0]
-    for sb in range(moments.shape[0] // terms):
-        if inter_ref is not None:
-            s = inter_ref[0] * z[0:1]
-            for r in range(1, modes):
-                s = s + inter_ref[r] * z[r : r + 1]
-            parts.append(s)
-        acc = cs_ref[0] * moments[sb * terms : sb * terms + 1]
-        for n in range(1, terms):
-            acc = acc + cs_ref[n] * moments[sb * terms + n : sb * terms + n + 1]
-        z = l16 * z + acc
+    if inter_ref is not None:
+        modes = z.shape[0]
+        for sb in range(subs):
+            parts.append(tree_sum([inter_ref[r] * zs[sb][r : r + 1] for r in range(modes)]))
     return z, parts
 
 
@@ -116,28 +126,34 @@
     o_ref[...] = (gate_ref[...].astype(jnp.float32) * total).astype(o_ref.dtype)
 
 
+def np_split(values):
+    high = values.astype(jnp.bfloat16)
+    low = (values - high.astype(np.float64)).astype(jnp.bfloat16)
+    return high, low
+
+
 def bases(rows):
     subs = rows // SUB
-    n = jnp.arange(TERMS, dtype=jnp.float32)
-    t = jnp.arange(rows)
-    sb, tl = t // SUB, (t % SUB).astype(jnp.float32)
+    n = np.arange(TERMS, dtype=np.float64)
+    t = np.arange(rows)
+    sb, tl = t // SUB, (t % SUB).astype(np.float64)
     same = sb[:, None] == sb[None, :]
-    lag = (t[:, None] - t[None, :]).astype(jnp.float32)
-    near = jnp.where(
+    lag = (t[:, None] - t[None, :]).astype(np.float64)
+    near = np.where(
         (same & (lag >= 0))[None], ((lag - 7.5) / 8.0)[None] ** n[:, None, None], 0.0
     ).reshape(TERMS * rows, rows)
-    own = jnp.arange(subs)[:, None] == sb[None, :]
-    mom = jnp.where(own[:, None, :], ((7.5 - tl) / 8.0)[None, None, :] ** n[None, :, None], 0.0)
+    own = np.arange(subs)[:, None] == sb[None, :]
+    mom = np.where(own[:, None, :], ((7.5 - tl) / 8.0)[None, None, :] ** n[None, :, None], 0.0)
     mom = mom.reshape(subs * TERMS, rows)
-    psi = jnp.where(own.T[:, :, None], ((tl - 7.5) / 8.0)[:, None, None] ** n[None, None, :], 0.0)
+    psi = np.where(own.T[:, :, None], ((tl - 7.5) / 8.0)[:, None, None] ** n[None, None, :], 0.0)
     psi = psi.reshape(rows, subs * TERMS)
-    nh, nl = split_pair(near)
-    mh, ml = split_pair(mom)
-    ph, pl_ = split_pair(psi)
+    nh, nl = np_split(near)
+    mh, ml = np_split(mom)
+    ph, pl_ = np_split(psi)
     return (
-        jnp.concatenate([nh, nl], 1),
-        jnp.concatenate([mh, ml], 1),
-        jnp.concatenate([ph, ph, pl_], 1),
+        jnp.asarray(np.concatenate([nh, nl], 1)),
+        jnp.asarray(np.concatenate([mh, ml], 1)),
+        jnp.asarray(np.concatenate([ph, ph, pl_], 1)),
     )
 
 

time: 118 us -> 115 us (0.975)
  other arithmetic: 9.49 us -> 5.2 us
  starting transfers between devices: 12.6 us -> 15.2 us
    ppermute x4, starting transfers between devices: 12.6 us -> 15.2 us  [passed_along(): return lax.ppermute(shard, axis, pairs)]
    concatenate x3 -> x0, other arithmetic: 2.21 us -> none  [the longest x1 0.87 us: bases(): jnp.concatenate([nh, nl], 1)]
    unnamed x7 -> x9, local copies, waits for them, and re-layouts: 10.2 us -> 10.3 us
  transfers between devices with their start and end apart: 4 -> 4, of which waited for: 2 -> 3; matrix products, arithmetic and copies ran while one was open for 20% -> 16% of each run, Pallas kernels for 0% -> 0%
where the time goes in v5:
time: 115 us
  Pallas kernels  74.3 us (65%)
  local copies, waits for them, and re-layouts  17.7 us (15%)
  starting transfers between devices  15.2 us (13%)
  other arithmetic  5.2 us (5%)
  waiting for transfers between devices  2.29 us (2%)
    pallas_call x1, Pallas kernels, long_conv_out(): pl.pallas_call(main_kernel, grid=grid, in_specs=[pl.BlockSpec((rows, lane...  30.6 us
    pallas_call x1, Pallas kernels, front(): pl.pallas_call(front_kernel, grid=(chans // lanes,), in_specs=[pl.BlockSp...  30.4 us
    ppermute x4, starting transfers between devices, passed_along(): return lax.ppermute(shard, axis, pairs)  15.2 us
    pallas_call x1, Pallas kernels, long_conv_out(): pl.pallas_call(state_kernel, grid=grid, in_specs=[pl.BlockSpec((rows, lan...  13.4 us
    unnamed x9, local copies, waits for them, and re-layouts  10.3 us
    squeeze x1, local copies, waits for them, and re-layouts, per_device(): return long_conv_out(lr_input, gates[0], lr_rate, lr_residue, lr_skip)  6.02 us
  transfers between devices with their start and end apart: 4, of which 3 were waited for; matrix products, arithmetic and copies ran while one was open for 16% of the time, Pallas kernels for 0%

profile of v5, /device:TPU:0, one launch (start us, length us, event | category | flops | bytes accessed | tf_op | source)
XLA Modules:
  0.0 114.8 jit_solution(11929973842837823085)
XLA Ops:
  0.0 1.2 %slice.12 = bf16[3,144,1024]{2,1,0:T(8,128)(2,1)S(1)} slice(bf16[3,2048,1024]{2,1,0:T(8,128)(2,1)} %bitcast.39), slice={[0:3], [1904:2048], [0:1024]} | slice | bytes 1769472 | tf_op jit(solution)/shard_map/slice | solution.py:306
  1.2 5.0 %collective-permute-start = (bf16[3,144,1024]{2,1,0:T(8,128)(2,1)S(1)}, bf16[3,144,1024]{2,1,0:T(8,128)(2,1)S(1)}, u32[]{:S(2)}, u32[]{:S(2)}) collective-permute-start(bf16[3,144,1024]{2,1,0:T(8,128)(2,1)S(1)} %slice.12), channel_id=1, source_target_pairs={{0,4},{4,8},{8,12},{1,5},{5,9},{9,13},{2,6},{6,10},{10,14},{3,7},{... | collective-permute-start | bytes 2654216 | tf_op jit(solution)/shard_map/ppermute | solution.py:20
  6.3 0.0 copy-start.3
  6.3 0.0 copy-start.1
  6.3 0.0 copy-start.2
  6.3 9.3 %copy.13 = bf16[2048,2,1024]{2,0,1:T(8,128)(2,1)} copy(bf16[2048,2,1024]{2,1,0:T(2,128)(2,1)} %param.13) | data formatting | bytes 16777216 | tf_op args[3]
  15.6 0.0 copy-done.3
  15.6 0.1 rev.3
  15.7 0.1 pad.2.clone
  15.8 0.0 copy-done.1
  15.8 0.0 copy-done.2
  15.8 0.7 exponential_bitcast_fusion
  16.5 0.2 reduce-window.8
  16.7 1.6 %divide_multiply_fusion.1 = (f32[8,16,1024]{2,1,0:T(8,128)}, f32[8,1024]{1,0:T(8,128)}) fusion(f32[8]{0:T(128)S(1)} %bitcast.43, f32[16,1024]{1,0:T(8,128)S(1)} %get-tuple-element.12, f32[16,1024]{1,0:T(8,128)S(1)} %get-tuple-element.13, f32[16,1024]{1,0:T(8,128)S(1)} %get-tuple-element.14), kind=kLoop, calls=%fused_computation.5 | loop fusion | flops 516096 | bytes 753696 | tf_op jit(solution)/shard_map/mul | solution.py:172
  18.3 0.7 maximum_maximum_fusion.rows_ref
  19.0 6.0 %slice_bitcast_fusion = (bf16[2048,1024]{1,0:T(8,128)(2,1)}, bf16[2048,1024]{1,0:T(8,128)(2,1)}) fusion(bf16[2,2048,1024]{2,1,0:T(8,128)(2,1)} %bitcast.38), kind=kLoop, calls=%fused_computation.1 | loop fusion | bytes 16777216 | tf_op jit(solution)/shard_map/squeeze | solution.py:309
  25.0 0.1 collective-permute-done.halo_ref
  25.1 0.0 copy-start
  25.1 0.9 copy-done
  26.0 30.4 %shard_map.100.x_ref = bf16[2048,1024]{1,0:T(8,128)(2,1)} custom-call(bf16[3,2048,1024]{2,1,0:T(8,128)(2,1)} %bitcast.40, bf16[3,144,1024]{2,1,0:T(8,128)(2,1)} %copy-done, f32[3,7,1024]{2,1,0:T(8,128)} %bitcast.41, f32[64,256]{1,0:T(8,128)} %maximum_maximum_fusion.rows_ref, bf16[2048,1024]{1,0:T(8,128)(2,1)} %get-tuple-element.6.gate_ref), custom_call_target="tpu_custom_call" | custom-call | tf_op jit(solution)/shard_map/pallas_call | solution.py:283
  56.4 13.4 %shard_map.101 = f32[16,1024]{1,0:T(8,128)} custom-call(bf16[2048,1024]{1,0:T(8,128)(2,1)} %shard_map.100.x_ref, bf16[64,256]{1,0:T(8,128)(2,1)} %constant.10.clone.mom_ref, f32[8,16,1024]{2,1,0:T(8,128)} %get-tuple-element.7.cs_ref, f32[16,1024]{1,0:T(8,128)} %get-tuple-element.11.l16_ref), custom_call_target="tpu_custom_call" | custom-call | tf_op jit(solution)/shard_map/pallas_call | solution.py:181
  69.8 4.4 %collective-permute-start.1 = (f32[16,1024]{1,0:T(8,128)}, f32[16,1024]{1,0:T(8,128)S(1)}, u32[]{:S(2)}, u32[]{:S(2)}) collective-permute-start(f32[16,1024]{1,0:T(8,128)} %shard_map.101), channel_id=1, source_target_pairs={{0,4},{4,8},{8,12},{1,5},{5,9},{9,13},{2,6},{6,10},{10,14},{3,7},{... | collective-permute-start | bytes 196616 | tf_op jit(solution)/shard_map/ppermute | solution.py:20
  74.2 4.5 %collective-permute-start.2 = (f32[16,1024]{1,0:T(8,128)}, f32[16,1024]{1,0:T(8,128)S(1)}, u32[]{:S(2)}, u32[]{:S(2)}) collective-permute-start(f32[16,1024]{1,0:T(8,128)} %shard_map.101), channel_id=1, source_target_pairs={{0,8},{4,12},{1,9},{5,13},{2,10},{6,14},{3,11},{7,15},{16,24},{20,... | collective-permute-start | bytes 196616 | tf_op jit(solution)/shard_map/ppermute | solution.py:20
  78.7 1.3 %collective-permute-start.3 = (f32[16,1024]{1,0:T(8,128)}, f32[16,1024]{1,0:T(8,128)S(1)}, u32[]{:S(2)}, u32[]{:S(2)}) collective-permute-start(f32[16,1024]{1,0:T(8,128)} %shard_map.101), channel_id=1, source_target_pairs={{0,12},{1,13},{2,14},{3,15},{16,28},{17,29},{18,30},{19,31}} | collective-permute-start | bytes 196616 | tf_op jit(solution)/shard_map/ppermute | solution.py:20
  80.0 0.0 collective-permute-done.1
  80.0 0.9 collective-permute-done.2
  80.9 1.3 %collective-permute-done.3 = f32[16,1024]{1,0:T(8,128)S(1)} collective-permute-done((f32[16,1024]{1,0:T(8,128)}, f32[16,1024]{1,0:T(8,128)S(1)}, u32[]{:S(2)}, u32[]{:S(2)}) %collective-permute-start.3) | collective-permute-done | bytes 65568 | tf_op jit(solution)/shard_map/ppermute | solution.py:20
  82.2 0.7 fusion
  82.9 1.4 %divide_multiply_fusion.inter_ref = f32[16,8,1024]{2,1,0:T(8,128)} fusion(f32[8]{0:T(128)S(1)} %bitcast.44, f32[16,1024]{1,0:T(8,128)S(1)} %get-tuple-element.12, f32[16,1024]{1,0:T(8,128)S(1)} %get-tuple-element.10), kind=kLoop, calls=%fused_computation.3 | loop fusion | flops 262144 | bytes 655392 | tf_op jit(solution)/shard_map/mul | solution.py:174
  84.2 30.6 %shard_map.102 = bf16[2048,1024]{1,0:T(8,128)(2,1)} custom-call(bf16[2048,1024]{1,0:T(8,128)(2,1)} %shard_map.100.x_ref, bf16[2048,1024]{1,0:T(8,128)(2,1)} %get-tuple-element.5.gate_ref, bf16[1024,256]{1,0:T(8,128)(2,1)} %constant.9.clone.phi_ref, bf16[64,256]{1,0:T(8,128)(2,1)} %constant.10.clone.mom_ref, bf16[128,192]{1,0:T(8,128)(2,1)} %constant.30.clone.psi_ref, ...), custom_call_target="tpu_custom_call" | custom-call | tf_op jit(solution)/shard_map/pallas_call | solution.py:202
  (4 shorter events, 0.0 us)
Async XLA Ops:
  1.2 23.9 %collective-permute-start = (bf16[3,144,1024]{2,1,0:T(8,128)(2,1)S(1)}, bf16[3,144,1024]{2,1,0:T(8,128)(2,1)S(1)}, u32[]{:S(2)}, u32[]{:S(2)}) collective-permute-start(bf16[3,144,1024]{2,1,0:T(8,128)(2,1)S(1)} %slice.12), channel_id=1, source_target_pairs={{0,4},{4,8},{8,12},{1,5},{5,9},{9,13},{2,6},{6,10},{10,14},{3,7},{... | collective-permute-start | bytes 2654216 | tf_op jit(solution)/shard_map/ppermute | solution.py:20
  6.3 9.4 %copy-start.3 = (bf16[64,128]{1,0:T(8,128)(2,1)S(1)}, bf16[64,128]{1,0:T(8,128)(2,1)}, u32[]{:S(2)}) copy-start(bf16[64,128]{1,0:T(8,128)(2,1)} %param.12) | copy-start | bytes 49156
  6.3 9.6 %copy-start.1 = (f32[1024,16]{0,1:T(8,128)S(1)}, f32[1024,16]{0,1:T(8,128)}, u32[]{:S(2)}) copy-start(f32[1024,16]{0,1:T(8,128)} %param.14) | copy-start | bytes 196612
  6.3 9.5 %copy-start.2 = (f32[1024,16]{0,1:T(8,128)S(1)}, f32[1024,16]{0,1:T(8,128)}, u32[]{:S(2)}) copy-start(f32[1024,16]{0,1:T(8,128)} %param.15) | copy-start | bytes 196612
  25.1 0.9 copy-start
  69.8 10.2 %collective-permute-start.1 = (f32[16,1024]{1,0:T(8,128)}, f32[16,1024]{1,0:T(8,128)S(1)}, u32[]{:S(2)}, u32[]{:S(2)}) collective-permute-start(f32[16,1024]{1,0:T(8,128)} %shard_map.101), channel_id=1, source_target_pairs={{0,4},{4,8},{8,12},{1,5},{5,9},{9,13},{2,6},{6,10},{10,14},{3,7},{... | collective-permute-start | bytes 196616 | tf_op jit(solution)/shard_map/ppermute | solution.py:20
  74.2 6.7 %collective-permute-start.2 = (f32[16,1024]{1,0:T(8,128)}, f32[16,1024]{1,0:T(8,128)S(1)}, u32[]{:S(2)}, u32[]{:S(2)}) collective-permute-start(f32[16,1024]{1,0:T(8,128)} %shard_map.101), channel_id=1, source_target_pairs={{0,8},{4,12},{1,9},{5,13},{2,10},{6,14},{3,11},{7,15},{16,24},{20,... | collective-permute-start | bytes 196616 | tf_op jit(solution)/shard_map/ppermute | solution.py:20
  78.7 3.5 %collective-permute-start.3 = (f32[16,1024]{1,0:T(8,128)}, f32[16,1024]{1,0:T(8,128)S(1)}, u32[]{:S(2)}, u32[]{:S(2)}) collective-permute-start(f32[16,1024]{1,0:T(8,128)} %shard_map.101), channel_id=1, source_target_pairs={{0,12},{1,13},{2,14},{3,15},{16,28},{17,29},{18,30},{19,31}} | collective-permute-start | bytes 196616 | tf_op jit(solution)/shard_map/ppermute | solution.py:20

commit v6 on v5

--- a/solution.py
+++ b/solution.py
@@ -123,7 +123,7 @@
     high, low = split_pair(jnp.concatenate(parts, 0))
     far = jnp.dot(psi_ref[...], jnp.concatenate([high, low, high], 0), preferred_element_type=jnp.float32)
     total = y + far + skip_ref[...] * xb.astype(jnp.float32)
-    o_ref[...] = (gate_ref[...].astype(jnp.float32) * total).astype(o_ref.dtype)
+    o_ref[...] = (gate_ref[:, 0, :].astype(jnp.float32) * total).astype(o_ref.dtype)
 
 
 def np_split(values):
@@ -204,7 +204,7 @@
         grid=grid,
         in_specs=[
             pl.BlockSpec((rows, lanes), lambda j, b: (b, j)),
-            pl.BlockSpec((rows, lanes), lambda j, b: (b, j)),
+            pl.BlockSpec((rows, 2, lanes), lambda j, b: (b, 0, j)),
             pl.BlockSpec((TERMS * rows, 2 * rows), lambda j, b: (0, 0)),
             pl.BlockSpec((subs_terms, 2 * rows), lambda j, b: (0, 0)),
             pl.BlockSpec((rows, 3 * subs_terms), lambda j, b: (0, 0)),
@@ -304,9 +304,8 @@
     count = features.shape[0]
     planes = features.transpose(1, 0, 2)
     halo = passed_along(planes[:, count - HALO :], "ctx", 1)
-    gates = lr_gates.transpose(1, 0, 2)
-    lr_input = front(planes, halo, short_filter, mr_filter, gates[1])
-    return long_conv_out(lr_input, gates[0], lr_rate, lr_residue, lr_skip)
+    lr_input = front(planes, halo, short_filter, mr_filter, lr_gates[:, 1, :])
+    return long_conv_out(lr_input, lr_gates, lr_rate, lr_residue, lr_skip)
 
 
 def solution(mesh):

time: 115 us -> 117 us (1.017)
  Pallas kernels: 74.3 us -> 76.4 us
    slice x0 -> x1, local copies, waits for them, and re-layouts: none -> 10.3 us  [per_device(): lr_input = front(planes, halo, short_filter, mr_filter, lr_gates[:, 1, :])]
    squeeze x1 -> x0, local copies, waits for them, and re-layouts: 6.02 us -> none  [per_device(): return long_conv_out(lr_input, gates[0], lr_rate, lr_residue, lr_skip)]
    unnamed x9 -> x7, local copies, waits for them, and re-layouts: 10.3 us -> 4.65 us
    pallas_call x1, Pallas kernels: 30.6 us -> 32.7 us  [long_conv_out(): pl.pallas_call(main_kernel, grid=grid, in_specs=[pl.BlockSpec((rows, lane...]
  transfers between devices with their start and end apart: 4 -> 4, of which waited for: 3 -> 3; matrix products, arithmetic and copies ran while one was open for 16% -> 15% of each run, Pallas kernels for 0% -> 0%
where the time goes in v6:
time: 117 us
  Pallas kernels  76.4 us (65%)
  local copies, waits for them, and re-layouts  17 us (15%)
  starting transfers between devices  15.2 us (13%)
  other arithmetic  5.23 us (4%)
  waiting for transfers between devices  2.96 us (3%)
    pallas_call x1, Pallas kernels, long_conv_out(): pl.pallas_call(main_kernel, grid=grid, in_specs=[pl.BlockSpec((rows, lane...  32.7 us
    pallas_call x1, Pallas kernels, front(): pl.pallas_call(front_kernel, grid=(chans // lanes,), in_specs=[pl.BlockSp...  30.4 us
    ppermute x4, starting transfers between devices, passed_along(): return lax.ppermute(shard, axis, pairs)  15.2 us
    pallas_call x1, Pallas kernels, long_conv_out(): pl.pallas_call(state_kernel, grid=grid, in_specs=[pl.BlockSpec((rows, lan...  13.4 us
    slice x1, local copies, waits for them, and re-layouts, per_device(): lr_input = front(planes, halo, short_filter, mr_filter, lr_gates[:, 1, :])  10.3 us
    unnamed x7, local copies, waits for them, and re-layouts  4.65 us
    ppermute x4, waiting for transfers between devices, passed_along(): return lax.ppermute(shard, axis, pairs)  2.96 us
  transfers between devices with their start and end apart: 4, of which 3 were waited for; matrix products, arithmetic and copies ran while one was open for 15% of the time, Pallas kernels for 0%

profile of v6, /device:TPU:0, one launch (start us, length us, event | category | flops | bytes accessed | tf_op | source)
XLA Modules:
  0.0 116.9 jit_solution(10826346088288014529)
XLA Ops:
  0.0 1.2 %slice.8 = bf16[3,144,1024]{2,1,0:T(8,128)(2,1)S(1)} slice(bf16[3,2048,1024]{2,1,0:T(8,128)(2,1)} %bitcast.35), slice={[0:3], [1904:2048], [0:1024]} | slice | bytes 1769472 | tf_op jit(solution)/shard_map/slice | solution.py:306
  1.2 5.0 %collective-permute-start = (bf16[3,144,1024]{2,1,0:T(8,128)(2,1)S(1)}, bf16[3,144,1024]{2,1,0:T(8,128)(2,1)S(1)}, u32[]{:S(2)}, u32[]{:S(2)}) collective-permute-start(bf16[3,144,1024]{2,1,0:T(8,128)(2,1)S(1)} %slice.8), channel_id=1, source_target_pairs={{0,4},{4,8},{8,12},{1,5},{5,9},{9,13},{2,6},{6,10},{10,14},{3,7},{... | collective-permute-start | bytes 2654216 | tf_op jit(solution)/shard_map/ppermute | solution.py:20
  6.2 0.8 rev.3
  7.1 0.1 pad.2.clone
  7.1 10.3 %slice.7 = bf16[2048,1,1024]{2,1,0:T(2,128)(2,1)S(1)} slice(bf16[2048,2,1024]{2,1,0:T(2,128)(2,1)} %gate_ref.1), slice={[0:2048], [1:2], [0:1024]} | slice | bytes 8388608 | tf_op jit(solution)/shard_map/slice | solution.py:307
  17.4 0.0 copy-start.1
  17.4 0.0 copy-start.2
  17.4 3.7 %copy.14 = bf16[2048,1,1024]{2,0,1:T(8,128)(2,1)} copy(bf16[2048,1,1024]{2,1,0:T(2,128)(2,1)S(1)} %slice.7) | data formatting | bytes 8388608
  21.2 0.2 reduce-window.8
  21.4 0.7 maximum_maximum_fusion.rows_ref
  22.1 0.0 copy-done.1
  22.1 0.0 copy-done.2
  22.1 0.7 exponential_bitcast_fusion
  22.7 1.6 %divide_multiply_fusion.1 = (f32[8,16,1024]{2,1,0:T(8,128)}, f32[8,1024]{1,0:T(8,128)}) fusion(f32[8]{0:T(128)S(1)} %bitcast.39, f32[16,1024]{1,0:T(8,128)S(1)} %get-tuple-element.10, f32[16,1024]{1,0:T(8,128)S(1)} %get-tuple-element.11, f32[16,1024]{1,0:T(8,128)S(1)} %get-tuple-element.12), kind=kLoop, calls=%fused_computation.3 | loop fusion | flops 516096 | bytes 753696 | tf_op jit(solution)/shard_map/mul | solution.py:172
  24.3 0.8 collective-permute-done.halo_ref
  25.1 0.0 copy-start
  25.1 0.9 copy-done
  26.0 30.4 %shard_map.100.x_ref = bf16[2048,1024]{1,0:T(8,128)(2,1)} custom-call(bf16[3,2048,1024]{2,1,0:T(8,128)(2,1)} %bitcast.36, bf16[3,144,1024]{2,1,0:T(8,128)(2,1)} %copy-done, f32[3,7,1024]{2,1,0:T(8,128)} %bitcast.37, f32[64,256]{1,0:T(8,128)} %maximum_maximum_fusion.rows_ref, bf16[2048,1024]{1,0:T(8,128)(2,1)} %bitcast.34), custom_call_target="tpu_custom_call" | custom-call | tf_op jit(solution)/shard_map/pallas_call | solution.py:283
  56.4 13.4 %shard_map.101 = f32[16,1024]{1,0:T(8,128)} custom-call(bf16[2048,1024]{1,0:T(8,128)(2,1)} %shard_map.100.x_ref, bf16[64,256]{1,0:T(8,128)(2,1)} %constant.10.clone.mom_ref, f32[8,16,1024]{2,1,0:T(8,128)} %get-tuple-element.5.cs_ref, f32[16,1024]{1,0:T(8,128)} %get-tuple-element.9.l16_ref), custom_call_target="tpu_custom_call" | custom-call | tf_op jit(solution)/shard_map/pallas_call | solution.py:181
  69.8 6.4 %collective-permute-start.3 = (f32[16,1024]{1,0:T(8,128)}, f32[16,1024]{1,0:T(8,128)S(1)}, u32[]{:S(2)}, u32[]{:S(2)}) collective-permute-start(f32[16,1024]{1,0:T(8,128)} %shard_map.101), channel_id=1, source_target_pairs={{0,12},{1,13},{2,14},{3,15},{16,28},{17,29},{18,30},{19,31}} | collective-permute-start | bytes 196616 | tf_op jit(solution)/shard_map/ppermute | solution.py:20
  76.2 1.3 %collective-permute-start.2 = (f32[16,1024]{1,0:T(8,128)}, f32[16,1024]{1,0:T(8,128)S(1)}, u32[]{:S(2)}, u32[]{:S(2)}) collective-permute-start(f32[16,1024]{1,0:T(8,128)} %shard_map.101), channel_id=1, source_target_pairs={{0,8},{4,12},{1,9},{5,13},{2,10},{6,14},{3,11},{7,15},{16,24},{20,... | collective-permute-start | bytes 196616 | tf_op jit(solution)/shard_map/ppermute | solution.py:20
  77.5 2.5 %collective-permute-start.1 = (f32[16,1024]{1,0:T(8,128)}, f32[16,1024]{1,0:T(8,128)S(1)}, u32[]{:S(2)}, u32[]{:S(2)}) collective-permute-start(f32[16,1024]{1,0:T(8,128)} %shard_map.101), channel_id=1, source_target_pairs={{0,4},{4,8},{8,12},{1,5},{5,9},{9,13},{2,6},{6,10},{10,14},{3,7},{... | collective-permute-start | bytes 196616 | tf_op jit(solution)/shard_map/ppermute | solution.py:20
  80.0 0.0 collective-permute-done.3
  80.0 0.1 collective-permute-done.2
  80.0 2.1 %collective-permute-done.1 = f32[16,1024]{1,0:T(8,128)S(1)} collective-permute-done((f32[16,1024]{1,0:T(8,128)}, f32[16,1024]{1,0:T(8,128)S(1)}, u32[]{:S(2)}, u32[]{:S(2)}) %collective-permute-start.1) | collective-permute-done | bytes 65568 | tf_op jit(solution)/shard_map/ppermute | solution.py:20
  82.2 0.7 fusion
  82.9 1.4 %divide_multiply_fusion.inter_ref = f32[16,8,1024]{2,1,0:T(8,128)} fusion(f32[8]{0:T(128)S(1)} %bitcast.40, f32[16,1024]{1,0:T(8,128)S(1)} %get-tuple-element.10, f32[16,1024]{1,0:T(8,128)S(1)} %get-tuple-element.8), kind=kLoop, calls=%fused_computation.1 | loop fusion | flops 262144 | bytes 655392 | tf_op jit(solution)/shard_map/mul | solution.py:174
  84.2 32.7 %shard_map.102 = bf16[2048,1024]{1,0:T(8,128)(2,1)} custom-call(bf16[2048,1024]{1,0:T(8,128)(2,1)} %shard_map.100.x_ref, bf16[2048,2,1024]{2,1,0:T(2,128)(2,1)} %gate_ref.1, bf16[1024,256]{1,0:T(8,128)(2,1)} %constant.9.clone.phi_ref, bf16[64,256]{1,0:T(8,128)(2,1)} %constant.10.clone.mom_ref, bf16[128,192]{1,0:T(8,128)(2,1)} %constant.30.clone.psi_ref, ...), custom_call_target="tpu_custom_call" | custom-call | tf_op jit(solution)/shard_map/pallas_call | solution.py:202
  (4 shorter events, 0.0 us)
Async XLA Ops:
  1.2 23.9 %collective-permute-start = (bf16[3,144,1024]{2,1,0:T(8,128)(2,1)S(1)}, bf16[3,144,1024]{2,1,0:T(8,128)(2,1)S(1)}, u32[]{:S(2)}, u32[]{:S(2)}) collective-permute-start(bf16[3,144,1024]{2,1,0:T(8,128)(2,1)S(1)} %slice.8), channel_id=1, source_target_pairs={{0,4},{4,8},{8,12},{1,5},{5,9},{9,13},{2,6},{6,10},{10,14},{3,7},{... | collective-permute-start | bytes 2654216 | tf_op jit(solution)/shard_map/ppermute | solution.py:20
  17.4 4.7 %copy-start.1 = (f32[1024,16]{0,1:T(8,128)S(1)}, f32[1024,16]{0,1:T(8,128)}, u32[]{:S(2)}) copy-start(f32[1024,16]{0,1:T(8,128)} %param.14) | copy-start | bytes 196612
  17.4 4.7 %copy-start.2 = (f32[1024,16]{0,1:T(8,128)S(1)}, f32[1024,16]{0,1:T(8,128)}, u32[]{:S(2)}) copy-start(f32[1024,16]{0,1:T(8,128)} %param.15) | copy-start | bytes 196612
  25.1 0.9 copy-start
  69.8 10.2 %collective-permute-start.3 = (f32[16,1024]{1,0:T(8,128)}, f32[16,1024]{1,0:T(8,128)S(1)}, u32[]{:S(2)}, u32[]{:S(2)}) collective-permute-start(f32[16,1024]{1,0:T(8,128)} %shard_map.101), channel_id=1, source_target_pairs={{0,12},{1,13},{2,14},{3,15},{16,28},{17,29},{18,30},{19,31}} | collective-permute-start | bytes 196616 | tf_op jit(solution)/shard_map/ppermute | solution.py:20
  76.2 3.9 %collective-permute-start.2 = (f32[16,1024]{1,0:T(8,128)}, f32[16,1024]{1,0:T(8,128)S(1)}, u32[]{:S(2)}, u32[]{:S(2)}) collective-permute-start(f32[16,1024]{1,0:T(8,128)} %shard_map.101), channel_id=1, source_target_pairs={{0,8},{4,12},{1,9},{5,13},{2,10},{6,14},{3,11},{7,15},{16,24},{20,... | collective-permute-start | bytes 196616 | tf_op jit(solution)/shard_map/ppermute | solution.py:20
  77.5 4.7 %collective-permute-start.1 = (f32[16,1024]{1,0:T(8,128)}, f32[16,1024]{1,0:T(8,128)S(1)}, u32[]{:S(2)}, u32[]{:S(2)}) collective-permute-start(f32[16,1024]{1,0:T(8,128)} %shard_map.101), channel_id=1, source_target_pairs={{0,4},{4,8},{8,12},{1,5},{5,9},{9,13},{2,6},{6,10},{10,14},{3,7},{... | collective-permute-start | bytes 196616 | tf_op jit(solution)/shard_map/ppermute | solution.py:20

commit v7 on v5

--- a/solution.py
+++ b/solution.py
@@ -10,7 +10,7 @@
 
 TAPS = 128
 SHORT = 7
-BLOCK = 128
+BLOCK = 256
 LANES = 1024
 
 

time: 115 us -> 121 us (1.052)
  Pallas kernels: 74.3 us -> 80.7 us
    pallas_call x1, Pallas kernels: 30.6 us -> 40.4 us  [long_conv_out(): pl.pallas_call(main_kernel, grid=grid, in_specs=[pl.BlockSpec((rows, lane...]
    pallas_call x1, Pallas kernels: 13.4 us -> 9.86 us  [long_conv_out(): pl.pallas_call(state_kernel, grid=grid, in_specs=[pl.BlockSpec((rows, lan...]
  transfers between devices with their start and end apart: 4 -> 4, of which waited for: 3 -> 3; matrix products, arithmetic and copies ran while one was open for 16% -> 15% of each run, Pallas kernels for 0% -> 0%
where the time goes in v7:
time: 121 us
  Pallas kernels  80.7 us (67%)
  local copies, waits for them, and re-layouts  17.7 us (15%)
  starting transfers between devices  15.3 us (13%)
  other arithmetic  5.2 us (4%)
  waiting for transfers between devices  2.11 us (2%)
    pallas_call x1, Pallas kernels, long_conv_out(): pl.pallas_call(main_kernel, grid=grid, in_specs=[pl.BlockSpec((rows, lane...  40.4 us
    pallas_call x1, Pallas kernels, front(): pl.pallas_call(front_kernel, grid=(chans // lanes,), in_specs=[pl.BlockSp...  30.4 us
    ppermute x4, starting transfers between devices, passed_along(): return lax.ppermute(shard, axis, pairs)  15.3 us
    unnamed x9, local copies, waits for them, and re-layouts  10.3 us
    pallas_call x1, Pallas kernels, long_conv_out(): pl.pallas_call(state_kernel, grid=grid, in_specs=[pl.BlockSpec((rows, lan...  9.86 us
    squeeze x1, local copies, waits for them, and re-layouts, per_device(): return long_conv_out(lr_input, gates[0], lr_rate, lr_residue, lr_skip)  6.02 us
  transfers between devices with their start and end apart: 4, of which 3 were waited for; matrix products, arithmetic and copies ran while one was open for 15% of the time, Pallas kernels for 0%

profile of v7, /device:TPU:0, one launch (start us, length us, event | category | flops | bytes accessed | tf_op | source)
XLA Modules:
  0.0 121.1 jit_solution(11219337810799375924)
XLA Ops:
  0.0 1.2 %slice.12 = bf16[3,144,1024]{2,1,0:T(8,128)(2,1)S(1)} slice(bf16[3,2048,1024]{2,1,0:T(8,128)(2,1)} %bitcast.39), slice={[0:3], [1904:2048], [0:1024]} | slice | bytes 1769472 | tf_op jit(solution)/shard_map/slice | solution.py:306
  1.2 5.0 %collective-permute-start = (bf16[3,144,1024]{2,1,0:T(8,128)(2,1)S(1)}, bf16[3,144,1024]{2,1,0:T(8,128)(2,1)S(1)}, u32[]{:S(2)}, u32[]{:S(2)}) collective-permute-start(bf16[3,144,1024]{2,1,0:T(8,128)(2,1)S(1)} %slice.12), channel_id=1, source_target_pairs={{0,4},{4,8},{8,12},{1,5},{5,9},{9,13},{2,6},{6,10},{10,14},{3,7},{... | collective-permute-start | bytes 2654216 | tf_op jit(solution)/shard_map/ppermute | solution.py:20
  6.3 0.0 copy-start.3
  6.3 0.0 copy-start.1
  6.3 0.0 copy-start.2
  6.3 9.3 %copy.13 = bf16[2048,2,1024]{2,0,1:T(8,128)(2,1)} copy(bf16[2048,2,1024]{2,1,0:T(2,128)(2,1)} %param.13) | data formatting | bytes 16777216 | tf_op args[3]
  15.6 0.0 copy-done.3
  15.6 0.1 rev.3
  15.7 0.1 pad.2.clone
  15.8 0.0 copy-done.1
  15.8 0.0 copy-done.2
  15.8 0.7 exponential_bitcast_fusion
  16.5 0.2 reduce-window.8
  16.7 1.6 %divide_multiply_fusion.1 = (f32[8,16,1024]{2,1,0:T(8,128)}, f32[8,1024]{1,0:T(8,128)}) fusion(f32[8]{0:T(128)S(1)} %bitcast.43, f32[16,1024]{1,0:T(8,128)S(1)} %get-tuple-element.12, f32[16,1024]{1,0:T(8,128)S(1)} %get-tuple-element.13, f32[16,1024]{1,0:T(8,128)S(1)} %get-tuple-element.14), kind=kLoop, calls=%fused_computation.5 | loop fusion | flops 516096 | bytes 753696 | tf_op jit(solution)/shard_map/mul | solution.py:172
  18.3 0.7 maximum_maximum_fusion.rows_ref
  19.0 6.0 %slice_bitcast_fusion = (bf16[2048,1024]{1,0:T(8,128)(2,1)}, bf16[2048,1024]{1,0:T(8,128)(2,1)}) fusion(bf16[2,2048,1024]{2,1,0:T(8,128)(2,1)} %bitcast.38), kind=kLoop, calls=%fused_computation.1 | loop fusion | bytes 16777216 | tf_op jit(solution)/shard_map/squeeze | solution.py:309
  25.0 0.1 collective-permute-done.halo_ref
  25.1 0.0 copy-start
  25.1 0.9 copy-done
  26.0 30.4 %shard_map.100.x_ref = bf16[2048,1024]{1,0:T(8,128)(2,1)} custom-call(bf16[3,2048,1024]{2,1,0:T(8,128)(2,1)} %bitcast.40, bf16[3,144,1024]{2,1,0:T(8,128)(2,1)} %copy-done, f32[3,7,1024]{2,1,0:T(8,128)} %bitcast.41, f32[64,256]{1,0:T(8,128)} %maximum_maximum_fusion.rows_ref, bf16[2048,1024]{1,0:T(8,128)(2,1)} %get-tuple-element.6.gate_ref), custom_call_target="tpu_custom_call" | custom-call | tf_op jit(solution)/shard_map/pallas_call | solution.py:283
  56.4 9.9 %shard_map.101 = f32[16,1024]{1,0:T(8,128)} custom-call(bf16[2048,1024]{1,0:T(8,128)(2,1)} %shard_map.100.x_ref, bf16[128,512]{1,0:T(8,128)(2,1)} %constant.10.clone.mom_ref, f32[8,16,1024]{2,1,0:T(8,128)} %get-tuple-element.7.cs_ref, f32[16,1024]{1,0:T(8,128)} %get-tuple-element.11.l16_ref), custom_call_target="tpu_custom_call" | custom-call | tf_op jit(solution)/shard_map/pallas_call | solution.py:181
  66.2 4.4 %collective-permute-start.1 = (f32[16,1024]{1,0:T(8,128)}, f32[16,1024]{1,0:T(8,128)S(1)}, u32[]{:S(2)}, u32[]{:S(2)}) collective-permute-start(f32[16,1024]{1,0:T(8,128)} %shard_map.101), channel_id=1, source_target_pairs={{0,4},{4,8},{8,12},{1,5},{5,9},{9,13},{2,6},{6,10},{10,14},{3,7},{... | collective-permute-start | bytes 196616 | tf_op jit(solution)/shard_map/ppermute | solution.py:20
  70.6 4.5 %collective-permute-start.2 = (f32[16,1024]{1,0:T(8,128)}, f32[16,1024]{1,0:T(8,128)S(1)}, u32[]{:S(2)}, u32[]{:S(2)}) collective-permute-start(f32[16,1024]{1,0:T(8,128)} %shard_map.101), channel_id=1, source_target_pairs={{0,8},{4,12},{1,9},{5,13},{2,10},{6,14},{3,11},{7,15},{16,24},{20,... | collective-permute-start | bytes 196616 | tf_op jit(solution)/shard_map/ppermute | solution.py:20
  75.1 1.5 %collective-permute-start.3 = (f32[16,1024]{1,0:T(8,128)}, f32[16,1024]{1,0:T(8,128)S(1)}, u32[]{:S(2)}, u32[]{:S(2)}) collective-permute-start(f32[16,1024]{1,0:T(8,128)} %shard_map.101), channel_id=1, source_target_pairs={{0,12},{1,13},{2,14},{3,15},{16,28},{17,29},{18,30},{19,31}} | collective-permute-start | bytes 196616 | tf_op jit(solution)/shard_map/ppermute | solution.py:20
  76.6 0.0 collective-permute-done.1
  76.6 0.7 collective-permute-done.2
  77.3 1.3 %collective-permute-done.3 = f32[16,1024]{1,0:T(8,128)S(1)} collective-permute-done((f32[16,1024]{1,0:T(8,128)}, f32[16,1024]{1,0:T(8,128)S(1)}, u32[]{:S(2)}, u32[]{:S(2)}) %collective-permute-start.3) | collective-permute-done | bytes 65568 | tf_op jit(solution)/shard_map/ppermute | solution.py:20
  78.6 0.7 fusion
  79.3 1.4 %divide_multiply_fusion.inter_ref = f32[16,8,1024]{2,1,0:T(8,128)} fusion(f32[8]{0:T(128)S(1)} %bitcast.44, f32[16,1024]{1,0:T(8,128)S(1)} %get-tuple-element.12, f32[16,1024]{1,0:T(8,128)S(1)} %get-tuple-element.10), kind=kLoop, calls=%fused_computation.3 | loop fusion | flops 262144 | bytes 655392 | tf_op jit(solution)/shard_map/mul | solution.py:174
  80.7 40.4 %shard_map.102 = bf16[2048,1024]{1,0:T(8,128)(2,1)} custom-call(bf16[2048,1024]{1,0:T(8,128)(2,1)} %shard_map.100.x_ref, bf16[2048,1024]{1,0:T(8,128)(2,1)} %get-tuple-element.5.gate_ref, bf16[2048,512]{1,0:T(8,128)(2,1)} %constant.9.clone.phi_ref, bf16[128,512]{1,0:T(8,128)(2,1)} %constant.10.clone.mom_ref, bf16[256,384]{1,0:T(8,128)(2,1)} %constant.30.clone.psi_ref, ...), custom_call_target="tpu_custom_call" | custom-call | tf_op jit(solution)/shard_map/pallas_call | solution.py:202
  (4 shorter events, 0.0 us)
Async XLA Ops:
  1.2 23.9 %collective-permute-start = (bf16[3,144,1024]{2,1,0:T(8,128)(2,1)S(1)}, bf16[3,144,1024]{2,1,0:T(8,128)(2,1)S(1)}, u32[]{:S(2)}, u32[]{:S(2)}) collective-permute-start(bf16[3,144,1024]{2,1,0:T(8,128)(2,1)S(1)} %slice.12), channel_id=1, source_target_pairs={{0,4},{4,8},{8,12},{1,5},{5,9},{9,13},{2,6},{6,10},{10,14},{3,7},{... | collective-permute-start | bytes 2654216 | tf_op jit(solution)/shard_map/ppermute | solution.py:20
  6.3 9.4 %copy-start.3 = (bf16[64,128]{1,0:T(8,128)(2,1)S(1)}, bf16[64,128]{1,0:T(8,128)(2,1)}, u32[]{:S(2)}) copy-start(bf16[64,128]{1,0:T(8,128)(2,1)} %param.12) | copy-start | bytes 49156
  6.3 9.6 %copy-start.1 = (f32[1024,16]{0,1:T(8,128)S(1)}, f32[1024,16]{0,1:T(8,128)}, u32[]{:S(2)}) copy-start(f32[1024,16]{0,1:T(8,128)} %param.14) | copy-start | bytes 196612
  6.3 9.5 %copy-start.2 = (f32[1024,16]{0,1:T(8,128)S(1)}, f32[1024,16]{0,1:T(8,128)}, u32[]{:S(2)}) copy-start(f32[1024,16]{0,1:T(8,128)} %param.15) | copy-start | bytes 196612
  25.1 0.9 copy-start
  66.2 10.4 %collective-permute-start.1 = (f32[16,1024]{1,0:T(8,128)}, f32[16,1024]{1,0:T(8,128)S(1)}, u32[]{:S(2)}, u32[]{:S(2)}) collective-permute-start(f32[16,1024]{1,0:T(8,128)} %shard_map.101), channel_id=1, source_target_pairs={{0,4},{4,8},{8,12},{1,5},{5,9},{9,13},{2,6},{6,10},{10,14},{3,7},{... | collective-permute-start | bytes 196616 | tf_op jit(solution)/shard_map/ppermute | solution.py:20
  70.6 6.7 %collective-permute-start.2 = (f32[16,1024]{1,0:T(8,128)}, f32[16,1024]{1,0:T(8,128)S(1)}, u32[]{:S(2)}, u32[]{:S(2)}) collective-permute-start(f32[16,1024]{1,0:T(8,128)} %shard_map.101), channel_id=1, source_target_pairs={{0,8},{4,12},{1,9},{5,13},{2,10},{6,14},{3,11},{7,15},{16,24},{20,... | collective-permute-start | bytes 196616 | tf_op jit(solution)/shard_map/ppermute | solution.py:20
  75.1 3.5 %collective-permute-start.3 = (f32[16,1024]{1,0:T(8,128)}, f32[16,1024]{1,0:T(8,128)S(1)}, u32[]{:S(2)}, u32[]{:S(2)}) collective-permute-start(f32[16,1024]{1,0:T(8,128)} %shard_map.101), channel_id=1, source_target_pairs={{0,12},{1,13},{2,14},{3,15},{16,28},{17,29},{18,30},{19,31}} | collective-permute-start | bytes 196616 | tf_op jit(solution)/shard_map/ppermute | solution.py:20

commit v8 on v5

--- a/solution.py
+++ b/solution.py
@@ -11,6 +11,7 @@
 TAPS = 128
 SHORT = 7
 BLOCK = 128
+STATE_BLOCK = 256
 LANES = 1024
 
 
@@ -178,12 +179,14 @@
     subs_terms = mom.shape[0]
     params = pltpu.CompilerParams(dimension_semantics=("arbitrary", "arbitrary"))
 
+    wide = min(STATE_BLOCK, count)
+    _, mom_wide, _ = bases(wide)
     final = pl.pallas_call(
         state_kernel,
-        grid=grid,
+        grid=(chans // lanes, count // wide),
         in_specs=[
-            pl.BlockSpec((rows, lanes), lambda j, b: (b, j)),
-            pl.BlockSpec((subs_terms, 2 * rows), lambda j, b: (0, 0)),
+            pl.BlockSpec((wide, lanes), lambda j, b: (b, j)),
+            pl.BlockSpec(mom_wide.shape, lambda j, b: (0, 0)),
             pl.BlockSpec((TERMS, modes, lanes), lambda j, b: (0, 0, j)),
             pl.BlockSpec((modes, lanes), lambda j, b: (0, j)),
         ],
@@ -191,7 +194,7 @@
         out_shape=jax.ShapeDtypeStruct((modes, chans), jnp.float32),
         scratch_shapes=[pltpu.VMEM((modes, lanes), jnp.float32)],
         compiler_params=params,
-    )(lr_input, mom, cs, l16)
+    )(lr_input, mom_wide, cs, l16)
 
     devices = lax.axis_size("ctx")
     incoming = jnp.zeros_like(final)

time: 115 us -> 112 us (0.974)
  Pallas kernels: 74.3 us -> 70.8 us
    pallas_call x1, Pallas kernels: 13.4 us -> 9.86 us  [long_conv_out(): pl.pallas_call(state_kernel, grid=(chans // lanes, count // wide), in_spe...]
  transfers between devices with their start and end apart: 4 -> 4, of which waited for: 3 -> 3; matrix products, arithmetic and copies ran while one was open for 16% -> 17% of each run, Pallas kernels for 0% -> 0%
where the time goes in v8:
time: 112 us; the launch traced here: 111 us
  Pallas kernels  70.8 us (63%)
  local copies, waits for them, and re-layouts  17.7 us (16%)
  starting transfers between devices  15.2 us (14%)
  other arithmetic  5.2 us (5%)
  waiting for transfers between devices  2.29 us (2%)
    pallas_call x1, Pallas kernels, long_conv_out(): pl.pallas_call(main_kernel, grid=grid, in_specs=[pl.BlockSpec((rows, lane...  30.6 us
    pallas_call x1, Pallas kernels, front(): pl.pallas_call(front_kernel, grid=(chans // lanes,), in_specs=[pl.BlockSp...  30.4 us
    ppermute x4, starting transfers between devices, passed_along(): return lax.ppermute(shard, axis, pairs)  15.2 us
    unnamed x9, local copies, waits for them, and re-layouts  10.3 us
    pallas_call x1, Pallas kernels, long_conv_out(): pl.pallas_call(state_kernel, grid=(chans // lanes, count // wide), in_spe...  9.86 us
    squeeze x1, local copies, waits for them, and re-layouts, per_device(): return long_conv_out(lr_input, gates[0], lr_rate, lr_residue, lr_skip)  6.02 us
    ppermute x4, waiting for transfers between devices, passed_along(): return lax.ppermute(shard, axis, pairs)  2.29 us
  transfers between devices with their start and end apart: 4, of which 3 were waited for; matrix products, arithmetic and copies ran while one was open for 17% of the time, Pallas kernels for 0%

profile of v8, /device:TPU:0, one launch (start us, length us, event | category | flops | bytes accessed | tf_op | source)
XLA Modules:
  0.0 111.2 jit_solution(16806079486751819837)
XLA Ops:
  0.0 1.2 %slice.12 = bf16[3,144,1024]{2,1,0:T(8,128)(2,1)S(1)} slice(bf16[3,2048,1024]{2,1,0:T(8,128)(2,1)} %bitcast.39), slice={[0:3], [1904:2048], [0:1024]} | slice | bytes 1769472 | tf_op jit(solution)/shard_map/slice | solution.py:309
  1.2 5.0 %collective-permute-start = (bf16[3,144,1024]{2,1,0:T(8,128)(2,1)S(1)}, bf16[3,144,1024]{2,1,0:T(8,128)(2,1)S(1)}, u32[]{:S(2)}, u32[]{:S(2)}) collective-permute-start(bf16[3,144,1024]{2,1,0:T(8,128)(2,1)S(1)} %slice.12), channel_id=1, source_target_pairs={{0,4},{4,8},{8,12},{1,5},{5,9},{9,13},{2,6},{6,10},{10,14},{3,7},{... | collective-permute-start | bytes 2654216 | tf_op jit(solution)/shard_map/ppermute | solution.py:21
  6.3 0.0 copy-start.3
  6.3 0.0 copy-start.1
  6.3 0.0 copy-start.2
  6.3 9.3 %copy.14 = bf16[2048,2,1024]{2,0,1:T(8,128)(2,1)} copy(bf16[2048,2,1024]{2,1,0:T(2,128)(2,1)} %param.14) | data formatting | bytes 16777216 | tf_op args[3]
  15.6 0.0 copy-done.3
  15.6 0.1 rev.3
  15.7 0.1 pad.2.clone
  15.8 0.0 copy-done.1
  15.8 0.0 copy-done.2
  15.8 0.7 exponential_bitcast_fusion
  16.5 0.2 reduce-window.8
  16.7 1.6 %divide_multiply_fusion.1 = (f32[8,16,1024]{2,1,0:T(8,128)}, f32[8,1024]{1,0:T(8,128)}) fusion(f32[8]{0:T(128)S(1)} %bitcast.43, f32[16,1024]{1,0:T(8,128)S(1)} %get-tuple-element.12, f32[16,1024]{1,0:T(8,128)S(1)} %get-tuple-element.13, f32[16,1024]{1,0:T(8,128)S(1)} %get-tuple-element.14), kind=kLoop, calls=%fused_computation.5 | loop fusion | flops 516096 | bytes 753696 | tf_op jit(solution)/shard_map/mul | solution.py:173
  18.3 0.7 maximum_maximum_fusion.rows_ref
  19.0 6.0 %slice_bitcast_fusion = (bf16[2048,1024]{1,0:T(8,128)(2,1)}, bf16[2048,1024]{1,0:T(8,128)(2,1)}) fusion(bf16[2,2048,1024]{2,1,0:T(8,128)(2,1)} %bitcast.38), kind=kLoop, calls=%fused_computation.1 | loop fusion | bytes 16777216 | tf_op jit(solution)/shard_map/squeeze | solution.py:312
  25.0 0.1 collective-permute-done.halo_ref
  25.1 0.0 copy-start
  25.1 0.9 copy-done
  26.0 30.4 %shard_map.109.x_ref = bf16[2048,1024]{1,0:T(8,128)(2,1)} custom-call(bf16[3,2048,1024]{2,1,0:T(8,128)(2,1)} %bitcast.40, bf16[3,144,1024]{2,1,0:T(8,128)(2,1)} %copy-done, f32[3,7,1024]{2,1,0:T(8,128)} %bitcast.41, f32[64,256]{1,0:T(8,128)} %maximum_maximum_fusion.rows_ref, bf16[2048,1024]{1,0:T(8,128)(2,1)} %get-tuple-element.6.gate_ref), custom_call_target="tpu_custom_call" | custom-call | tf_op jit(solution)/shard_map/pallas_call | solution.py:286
  56.4 9.9 %shard_map.110 = f32[16,1024]{1,0:T(8,128)} custom-call(bf16[2048,1024]{1,0:T(8,128)(2,1)} %shard_map.109.x_ref, bf16[128,512]{1,0:T(8,128)(2,1)} %constant.33.clone.mom_ref, f32[8,16,1024]{2,1,0:T(8,128)} %get-tuple-element.7.cs_ref, f32[16,1024]{1,0:T(8,128)} %get-tuple-element.11.l16_ref), custom_call_target="tpu_custom_call" | custom-call | tf_op jit(solution)/shard_map/pallas_call | solution.py:184
  66.2 4.4 %collective-permute-start.1 = (f32[16,1024]{1,0:T(8,128)}, f32[16,1024]{1,0:T(8,128)S(1)}, u32[]{:S(2)}, u32[]{:S(2)}) collective-permute-start(f32[16,1024]{1,0:T(8,128)} %shard_map.110), channel_id=1, source_target_pairs={{0,4},{4,8},{8,12},{1,5},{5,9},{9,13},{2,6},{6,10},{10,14},{3,7},{... | collective-permute-start | bytes 196616 | tf_op jit(solution)/shard_map/ppermute | solution.py:21
  70.6 4.5 %collective-permute-start.2 = (f32[16,1024]{1,0:T(8,128)}, f32[16,1024]{1,0:T(8,128)S(1)}, u32[]{:S(2)}, u32[]{:S(2)}) collective-permute-start(f32[16,1024]{1,0:T(8,128)} %shard_map.110), channel_id=1, source_target_pairs={{0,8},{4,12},{1,9},{5,13},{2,10},{6,14},{3,11},{7,15},{16,24},{20,... | collective-permute-start | bytes 196616 | tf_op jit(solution)/shard_map/ppermute | solution.py:21
  75.1 1.3 %collective-permute-start.3 = (f32[16,1024]{1,0:T(8,128)}, f32[16,1024]{1,0:T(8,128)S(1)}, u32[]{:S(2)}, u32[]{:S(2)}) collective-permute-start(f32[16,1024]{1,0:T(8,128)} %shard_map.110), channel_id=1, source_target_pairs={{0,12},{1,13},{2,14},{3,15},{16,28},{17,29},{18,30},{19,31}} | collective-permute-start | bytes 196616 | tf_op jit(solution)/shard_map/ppermute | solution.py:21
  76.4 0.0 collective-permute-done.1
  76.4 0.9 collective-permute-done.2
  77.3 1.3 %collective-permute-done.3 = f32[16,1024]{1,0:T(8,128)S(1)} collective-permute-done((f32[16,1024]{1,0:T(8,128)}, f32[16,1024]{1,0:T(8,128)S(1)}, u32[]{:S(2)}, u32[]{:S(2)}) %collective-permute-start.3) | collective-permute-done | bytes 65568 | tf_op jit(solution)/shard_map/ppermute | solution.py:21
  78.6 0.7 fusion
  79.3 1.4 %divide_multiply_fusion.inter_ref = f32[16,8,1024]{2,1,0:T(8,128)} fusion(f32[8]{0:T(128)S(1)} %bitcast.44, f32[16,1024]{1,0:T(8,128)S(1)} %get-tuple-element.12, f32[16,1024]{1,0:T(8,128)S(1)} %get-tuple-element.10), kind=kLoop, calls=%fused_computation.3 | loop fusion | flops 262144 | bytes 655392 | tf_op jit(solution)/shard_map/mul | solution.py:175
  80.7 30.6 %shard_map.111 = bf16[2048,1024]{1,0:T(8,128)(2,1)} custom-call(bf16[2048,1024]{1,0:T(8,128)(2,1)} %shard_map.109.x_ref, bf16[2048,1024]{1,0:T(8,128)(2,1)} %get-tuple-element.5.gate_ref, bf16[1024,256]{1,0:T(8,128)(2,1)} %constant.10.clone.phi_ref, bf16[64,256]{1,0:T(8,128)(2,1)} %constant.11.clone.mom_ref, bf16[128,192]{1,0:T(8,128)(2,1)} %constant.32.clone.psi_ref, ...), custom_call_target="tpu_custom_call" | custom-call | tf_op jit(solution)/shard_map/pallas_call | solution.py:205
  (4 shorter events, 0.0 us)
Async XLA Ops:
  1.2 23.9 %collective-permute-start = (bf16[3,144,1024]{2,1,0:T(8,128)(2,1)S(1)}, bf16[3,144,1024]{2,1,0:T(8,128)(2,1)S(1)}, u32[]{:S(2)}, u32[]{:S(2)}) collective-permute-start(bf16[3,144,1024]{2,1,0:T(8,128)(2,1)S(1)} %slice.12), channel_id=1, source_target_pairs={{0,4},{4,8},{8,12},{1,5},{5,9},{9,13},{2,6},{6,10},{10,14},{3,7},{... | collective-permute-start | bytes 2654216 | tf_op jit(solution)/shard_map/ppermute | solution.py:21
  6.3 9.4 %copy-start.3 = (bf16[64,128]{1,0:T(8,128)(2,1)S(1)}, bf16[64,128]{1,0:T(8,128)(2,1)}, u32[]{:S(2)}) copy-start(bf16[64,128]{1,0:T(8,128)(2,1)} %param.13) | copy-start | bytes 49156
  6.3 9.6 %copy-start.1 = (f32[1024,16]{0,1:T(8,128)S(1)}, f32[1024,16]{0,1:T(8,128)}, u32[]{:S(2)}) copy-start(f32[1024,16]{0,1:T(8,128)} %param.15) | copy-start | bytes 196612
  6.3 9.5 %copy-start.2 = (f32[1024,16]{0,1:T(8,128)S(1)}, f32[1024,16]{0,1:T(8,128)}, u32[]{:S(2)}) copy-start(f32[1024,16]{0,1:T(8,128)} %param.16) | copy-start | bytes 196612
  25.1 0.9 copy-start
  66.2 10.2 %collective-permute-start.1 = (f32[16,1024]{1,0:T(8,128)}, f32[16,1024]{1,0:T(8,128)S(1)}, u32[]{:S(2)}, u32[]{:S(2)}) collective-permute-start(f32[16,1024]{1,0:T(8,128)} %shard_map.110), channel_id=1, source_target_pairs={{0,4},{4,8},{8,12},{1,5},{5,9},{9,13},{2,6},{6,10},{10,14},{3,7},{... | collective-permute-start | bytes 196616 | tf_op jit(solution)/shard_map/ppermute | solution.py:21
  70.6 6.7 %collective-permute-start.2 = (f32[16,1024]{1,0:T(8,128)}, f32[16,1024]{1,0:T(8,128)S(1)}, u32[]{:S(2)}, u32[]{:S(2)}) collective-permute-start(f32[16,1024]{1,0:T(8,128)} %shard_map.110), channel_id=1, source_target_pairs={{0,8},{4,12},{1,9},{5,13},{2,10},{6,14},{3,11},{7,15},{16,24},{20,... | collective-permute-start | bytes 196616 | tf_op jit(solution)/shard_map/ppermute | solution.py:21
  75.1 3.5 %collective-permute-start.3 = (f32[16,1024]{1,0:T(8,128)}, f32[16,1024]{1,0:T(8,128)S(1)}, u32[]{:S(2)}, u32[]{:S(2)}) collective-permute-start(f32[16,1024]{1,0:T(8,128)} %shard_map.110), channel_id=1, source_target_pairs={{0,12},{1,13},{2,14},{3,15},{16,28},{17,29},{18,30},{19,31}} | collective-permute-start | bytes 196616 | tf_op jit(solution)/shard_map/ppermute | solution.py:21

commit v9 on v8

--- a/solution.py
+++ b/solution.py
@@ -11,7 +11,7 @@
 TAPS = 128
 SHORT = 7
 BLOCK = 128
-STATE_BLOCK = 256
+STATE_BLOCK = 512
 LANES = 1024
 
 

time: 112 us -> 112 us (level)
  no operation moved by 1% of the time
where the time goes in v9:
time: 112 us
  Pallas kernels  71.1 us (63%)
  local copies, waits for them, and re-layouts  17.7 us (16%)
  starting transfers between devices  15.2 us (14%)
  other arithmetic  5.2 us (5%)
  waiting for transfers between devices  2.29 us (2%)
    pallas_call x1, Pallas kernels, long_conv_out(): pl.pallas_call(main_kernel, grid=grid, in_specs=[pl.BlockSpec((rows, lane...  30.7 us
    pallas_call x1, Pallas kernels, front(): pl.pallas_call(front_kernel, grid=(chans // lanes,), in_specs=[pl.BlockSp...  30.4 us
    ppermute x4, starting transfers between devices, passed_along(): return lax.ppermute(shard, axis, pairs)  15.2 us
    unnamed x9, local copies, waits for them, and re-layouts  10.3 us
    pallas_call x1, Pallas kernels, long_conv_out(): pl.pallas_call(state_kernel, grid=(chans // lanes, count // wide), in_spe...  10 us
    squeeze x1, local copies, waits for them, and re-layouts, per_device(): return long_conv_out(lr_input, gates[0], lr_rate, lr_residue, lr_skip)  6.02 us
    ppermute x4, waiting for transfers between devices, passed_along(): return lax.ppermute(shard, axis, pairs)  2.29 us
  transfers between devices with their start and end apart: 4, of which 3 were waited for; matrix products, arithmetic and copies ran while one was open for 17% of the time, Pallas kernels for 0%

profile of v9, /device:TPU:0, one launch (start us, length us, event | category | flops | bytes accessed | tf_op | source)
XLA Modules:
  0.0 111.5 jit_solution(3921115904347029674)
XLA Ops:
  0.0 1.2 %slice.12 = bf16[3,144,1024]{2,1,0:T(8,128)(2,1)S(1)} slice(bf16[3,2048,1024]{2,1,0:T(8,128)(2,1)} %bitcast.39), slice={[0:3], [1904:2048], [0:1024]} | slice | bytes 1769472 | tf_op jit(solution)/shard_map/slice | solution.py:309
  1.2 5.0 %collective-permute-start = (bf16[3,144,1024]{2,1,0:T(8,128)(2,1)S(1)}, bf16[3,144,1024]{2,1,0:T(8,128)(2,1)S(1)}, u32[]{:S(2)}, u32[]{:S(2)}) collective-permute-start(bf16[3,144,1024]{2,1,0:T(8,128)(2,1)S(1)} %slice.12), channel_id=1, source_target_pairs={{0,4},{4,8},{8,12},{1,5},{5,9},{9,13},{2,6},{6,10},{10,14},{3,7},{... | collective-permute-start | bytes 2654216 | tf_op jit(solution)/shard_map/ppermute | solution.py:21
  6.3 0.0 copy-start.3
  6.3 0.0 copy-start.1
  6.3 0.0 copy-start.2
  6.3 9.3 %copy.14 = bf16[2048,2,1024]{2,0,1:T(8,128)(2,1)} copy(bf16[2048,2,1024]{2,1,0:T(2,128)(2,1)} %param.14) | data formatting | bytes 16777216 | tf_op args[3]
  15.6 0.0 copy-done.3
  15.6 0.1 rev.3
  15.7 0.1 pad.2.clone
  15.8 0.0 copy-done.1
  15.8 0.0 copy-done.2
  15.8 0.7 exponential_bitcast_fusion
  16.5 0.2 reduce-window.8
  16.7 1.6 %divide_multiply_fusion.1 = (f32[8,16,1024]{2,1,0:T(8,128)}, f32[8,1024]{1,0:T(8,128)}) fusion(f32[8]{0:T(128)S(1)} %bitcast.43, f32[16,1024]{1,0:T(8,128)S(1)} %get-tuple-element.12, f32[16,1024]{1,0:T(8,128)S(1)} %get-tuple-element.13, f32[16,1024]{1,0:T(8,128)S(1)} %get-tuple-element.14), kind=kLoop, calls=%fused_computation.5 | loop fusion | flops 516096 | bytes 753696 | tf_op jit(solution)/shard_map/mul | solution.py:173
  18.3 0.7 maximum_maximum_fusion.rows_ref
  19.0 6.0 %slice_bitcast_fusion = (bf16[2048,1024]{1,0:T(8,128)(2,1)}, bf16[2048,1024]{1,0:T(8,128)(2,1)}) fusion(bf16[2,2048,1024]{2,1,0:T(8,128)(2,1)} %bitcast.38), kind=kLoop, calls=%fused_computation.1 | loop fusion | bytes 16777216 | tf_op jit(solution)/shard_map/squeeze | solution.py:312
  25.0 0.1 collective-permute-done.halo_ref
  25.1 0.0 copy-start
  25.1 0.9 copy-done
  26.0 30.4 %shard_map.109.x_ref = bf16[2048,1024]{1,0:T(8,128)(2,1)} custom-call(bf16[3,2048,1024]{2,1,0:T(8,128)(2,1)} %bitcast.40, bf16[3,144,1024]{2,1,0:T(8,128)(2,1)} %copy-done, f32[3,7,1024]{2,1,0:T(8,128)} %bitcast.41, f32[64,256]{1,0:T(8,128)} %maximum_maximum_fusion.rows_ref, bf16[2048,1024]{1,0:T(8,128)(2,1)} %get-tuple-element.6.gate_ref), custom_call_target="tpu_custom_call" | custom-call | tf_op jit(solution)/shard_map/pallas_call | solution.py:286
  56.4 10.0 %shard_map.110 = f32[16,1024]{1,0:T(8,128)} custom-call(bf16[2048,1024]{1,0:T(8,128)(2,1)} %shard_map.109.x_ref, bf16[256,1024]{1,0:T(8,128)(2,1)} %constant.33.clone.mom_ref, f32[8,16,1024]{2,1,0:T(8,128)} %get-tuple-element.7.cs_ref, f32[16,1024]{1,0:T(8,128)} %get-tuple-element.11.l16_ref), custom_call_target="tpu_custom_call" | custom-call | tf_op jit(solution)/shard_map/pallas_call | solution.py:184
  66.4 4.4 %collective-permute-start.1 = (f32[16,1024]{1,0:T(8,128)}, f32[16,1024]{1,0:T(8,128)S(1)}, u32[]{:S(2)}, u32[]{:S(2)}) collective-permute-start(f32[16,1024]{1,0:T(8,128)} %shard_map.110), channel_id=1, source_target_pairs={{0,4},{4,8},{8,12},{1,5},{5,9},{9,13},{2,6},{6,10},{10,14},{3,7},{... | collective-permute-start | bytes 196616 | tf_op jit(solution)/shard_map/ppermute | solution.py:21
  70.8 4.5 %collective-permute-start.2 = (f32[16,1024]{1,0:T(8,128)}, f32[16,1024]{1,0:T(8,128)S(1)}, u32[]{:S(2)}, u32[]{:S(2)}) collective-permute-start(f32[16,1024]{1,0:T(8,128)} %shard_map.110), channel_id=1, source_target_pairs={{0,8},{4,12},{1,9},{5,13},{2,10},{6,14},{3,11},{7,15},{16,24},{20,... | collective-permute-start | bytes 196616 | tf_op jit(solution)/shard_map/ppermute | solution.py:21
  75.3 1.3 %collective-permute-start.3 = (f32[16,1024]{1,0:T(8,128)}, f32[16,1024]{1,0:T(8,128)S(1)}, u32[]{:S(2)}, u32[]{:S(2)}) collective-permute-start(f32[16,1024]{1,0:T(8,128)} %shard_map.110), channel_id=1, source_target_pairs={{0,12},{1,13},{2,14},{3,15},{16,28},{17,29},{18,30},{19,31}} | collective-permute-start | bytes 196616 | tf_op jit(solution)/shard_map/ppermute | solution.py:21
  76.6 0.0 collective-permute-done.1
  76.6 0.9 collective-permute-done.2
  77.5 1.3 %collective-permute-done.3 = f32[16,1024]{1,0:T(8,128)S(1)} collective-permute-done((f32[16,1024]{1,0:T(8,128)}, f32[16,1024]{1,0:T(8,128)S(1)}, u32[]{:S(2)}, u32[]{:S(2)}) %collective-permute-start.3) | collective-permute-done | bytes 65568 | tf_op jit(solution)/shard_map/ppermute | solution.py:21
  78.8 0.7 fusion
  79.5 1.4 %divide_multiply_fusion.inter_ref = f32[16,8,1024]{2,1,0:T(8,128)} fusion(f32[8]{0:T(128)S(1)} %bitcast.44, f32[16,1024]{1,0:T(8,128)S(1)} %get-tuple-element.12, f32[16,1024]{1,0:T(8,128)S(1)} %get-tuple-element.10), kind=kLoop, calls=%fused_computation.3 | loop fusion | flops 262144 | bytes 655392 | tf_op jit(solution)/shard_map/mul | solution.py:175
  80.8 30.7 %shard_map.111 = bf16[2048,1024]{1,0:T(8,128)(2,1)} custom-call(bf16[2048,1024]{1,0:T(8,128)(2,1)} %shard_map.109.x_ref, bf16[2048,1024]{1,0:T(8,128)(2,1)} %get-tuple-element.5.gate_ref, bf16[1024,256]{1,0:T(8,128)(2,1)} %constant.10.clone.phi_ref, bf16[64,256]{1,0:T(8,128)(2,1)} %constant.11.clone.mom_ref, bf16[128,192]{1,0:T(8,128)(2,1)} %constant.32.clone.psi_ref, ...), custom_call_target="tpu_custom_call" | custom-call | tf_op jit(solution)/shard_map/pallas_call | solution.py:205
  (4 shorter events, 0.0 us)
Async XLA Ops:
  1.2 23.9 %collective-permute-start = (bf16[3,144,1024]{2,1,0:T(8,128)(2,1)S(1)}, bf16[3,144,1024]{2,1,0:T(8,128)(2,1)S(1)}, u32[]{:S(2)}, u32[]{:S(2)}) collective-permute-start(bf16[3,144,1024]{2,1,0:T(8,128)(2,1)S(1)} %slice.12), channel_id=1, source_target_pairs={{0,4},{4,8},{8,12},{1,5},{5,9},{9,13},{2,6},{6,10},{10,14},{3,7},{... | collective-permute-start | bytes 2654216 | tf_op jit(solution)/shard_map/ppermute | solution.py:21
  6.3 9.4 %copy-start.3 = (bf16[64,128]{1,0:T(8,128)(2,1)S(1)}, bf16[64,128]{1,0:T(8,128)(2,1)}, u32[]{:S(2)}) copy-start(bf16[64,128]{1,0:T(8,128)(2,1)} %param.13) | copy-start | bytes 49156
  6.3 9.6 %copy-start.1 = (f32[1024,16]{0,1:T(8,128)S(1)}, f32[1024,16]{0,1:T(8,128)}, u32[]{:S(2)}) copy-start(f32[1024,16]{0,1:T(8,128)} %param.15) | copy-start | bytes 196612
  6.3 9.5 %copy-start.2 = (f32[1024,16]{0,1:T(8,128)S(1)}, f32[1024,16]{0,1:T(8,128)}, u32[]{:S(2)}) copy-start(f32[1024,16]{0,1:T(8,128)} %param.16) | copy-start | bytes 196612
  25.1 0.9 copy-start
  66.4 10.2 %collective-permute-start.1 = (f32[16,1024]{1,0:T(8,128)}, f32[16,1024]{1,0:T(8,128)S(1)}, u32[]{:S(2)}, u32[]{:S(2)}) collective-permute-start(f32[16,1024]{1,0:T(8,128)} %shard_map.110), channel_id=1, source_target_pairs={{0,4},{4,8},{8,12},{1,5},{5,9},{9,13},{2,6},{6,10},{10,14},{3,7},{... | collective-permute-start | bytes 196616 | tf_op jit(solution)/shard_map/ppermute | solution.py:21
  70.8 6.7 %collective-permute-start.2 = (f32[16,1024]{1,0:T(8,128)}, f32[16,1024]{1,0:T(8,128)S(1)}, u32[]{:S(2)}, u32[]{:S(2)}) collective-permute-start(f32[16,1024]{1,0:T(8,128)} %shard_map.110), channel_id=1, source_target_pairs={{0,8},{4,12},{1,9},{5,13},{2,10},{6,14},{3,11},{7,15},{16,24},{20,... | collective-permute-start | bytes 196616 | tf_op jit(solution)/shard_map/ppermute | solution.py:21
  75.3 3.5 %collective-permute-start.3 = (f32[16,1024]{1,0:T(8,128)}, f32[16,1024]{1,0:T(8,128)S(1)}, u32[]{:S(2)}, u32[]{:S(2)}) collective-permute-start(f32[16,1024]{1,0:T(8,128)} %shard_map.110), channel_id=1, source_target_pairs={{0,12},{1,13},{2,14},{3,15},{16,28},{17,29},{18,30},{19,31}} | collective-permute-start | bytes 196616 | tf_op jit(solution)/shard_map/ppermute | solution.py:21

commit v10 on v8

--- a/solution.py
+++ b/solution.py
@@ -115,9 +115,7 @@
     rows = xb.shape[0]
     x2 = jnp.concatenate([xb, xb], 0)
     near = jnp.dot(phi_ref[...], x2, preferred_element_type=jnp.float32)
-    y = ci_ref[0:1] * near[0:rows]
-    for n in range(1, ci_ref.shape[0]):
-        y = y + ci_ref[n : n + 1] * near[n * rows : (n + 1) * rows]
+    y = tree_sum([ci_ref[n : n + 1] * near[n * rows : (n + 1) * rows] for n in range(ci_ref.shape[0])])
     moments = jnp.dot(mom_ref[...], x2, preferred_element_type=jnp.float32)
     z, parts = carry_subblocks(moments, z_ref[...], cs_ref, l16_ref[...], inter_ref)
     z_ref[...] = z

time: 112 us -> 112 us (level)
  no operation moved by 1% of the time
where the time goes in v10:
time: 112 us; the launch traced here: 111 us
  Pallas kernels  70.8 us (63%)
  local copies, waits for them, and re-layouts  17.7 us (16%)
  starting transfers between devices  15.2 us (14%)
  other arithmetic  5.2 us (5%)
  waiting for transfers between devices  2.29 us (2%)
    pallas_call x1, Pallas kernels, long_conv_out(): pl.pallas_call(main_kernel, grid=grid, in_specs=[pl.BlockSpec((rows, lane...  30.6 us
    pallas_call x1, Pallas kernels, front(): pl.pallas_call(front_kernel, grid=(chans // lanes,), in_specs=[pl.BlockSp...  30.4 us
    ppermute x4, starting transfers between devices, passed_along(): return lax.ppermute(shard, axis, pairs)  15.2 us
    unnamed x9, local copies, waits for them, and re-layouts  10.3 us
    pallas_call x1, Pallas kernels, long_conv_out(): pl.pallas_call(state_kernel, grid=(chans // lanes, count // wide), in_spe...  9.86 us
    squeeze x1, local copies, waits for them, and re-layouts, per_device(): return long_conv_out(lr_input, gates[0], lr_rate, lr_residue, lr_skip)  6.02 us
    ppermute x4, waiting for transfers between devices, passed_along(): return lax.ppermute(shard, axis, pairs)  2.29 us
  transfers between devices with their start and end apart: 4, of which 3 were waited for; matrix products, arithmetic and copies ran while one was open for 17% of the time, Pallas kernels for 0%

profile of v10, /device:TPU:0, one launch (start us, length us, event | category | flops | bytes accessed | tf_op | source)
XLA Modules:
  0.0 111.3 jit_solution(8636282599597257484)
XLA Ops:
  0.0 1.2 %slice.12 = bf16[3,144,1024]{2,1,0:T(8,128)(2,1)S(1)} slice(bf16[3,2048,1024]{2,1,0:T(8,128)(2,1)} %bitcast.39), slice={[0:3], [1904:2048], [0:1024]} | slice | bytes 1769472 | tf_op jit(solution)/shard_map/slice | solution.py:307
  1.2 5.0 %collective-permute-start = (bf16[3,144,1024]{2,1,0:T(8,128)(2,1)S(1)}, bf16[3,144,1024]{2,1,0:T(8,128)(2,1)S(1)}, u32[]{:S(2)}, u32[]{:S(2)}) collective-permute-start(bf16[3,144,1024]{2,1,0:T(8,128)(2,1)S(1)} %slice.12), channel_id=1, source_target_pairs={{0,4},{4,8},{8,12},{1,5},{5,9},{9,13},{2,6},{6,10},{10,14},{3,7},{... | collective-permute-start | bytes 2654216 | tf_op jit(solution)/shard_map/ppermute | solution.py:21
  6.3 0.0 copy-start.3
  6.3 0.0 copy-start.1
  6.3 0.0 copy-start.2
  6.3 9.3 %copy.14 = bf16[2048,2,1024]{2,0,1:T(8,128)(2,1)} copy(bf16[2048,2,1024]{2,1,0:T(2,128)(2,1)} %param.14) | data formatting | bytes 16777216 | tf_op args[3]
  15.6 0.0 copy-done.3
  15.6 0.1 rev.3
  15.7 0.1 pad.2.clone
  15.8 0.0 copy-done.1
  15.8 0.0 copy-done.2
  15.8 0.7 exponential_bitcast_fusion
  16.5 0.2 reduce-window.8
  16.7 1.6 %divide_multiply_fusion.1 = (f32[8,16,1024]{2,1,0:T(8,128)}, f32[8,1024]{1,0:T(8,128)}) fusion(f32[8]{0:T(128)S(1)} %bitcast.43, f32[16,1024]{1,0:T(8,128)S(1)} %get-tuple-element.12, f32[16,1024]{1,0:T(8,128)S(1)} %get-tuple-element.13, f32[16,1024]{1,0:T(8,128)S(1)} %get-tuple-element.14), kind=kLoop, calls=%fused_computation.5 | loop fusion | flops 516096 | bytes 753696 | tf_op jit(solution)/shard_map/mul | solution.py:171
  18.3 0.7 maximum_maximum_fusion.rows_ref
  19.0 6.0 %slice_bitcast_fusion = (bf16[2048,1024]{1,0:T(8,128)(2,1)}, bf16[2048,1024]{1,0:T(8,128)(2,1)}) fusion(bf16[2,2048,1024]{2,1,0:T(8,128)(2,1)} %bitcast.38), kind=kLoop, calls=%fused_computation.1 | loop fusion | bytes 16777216 | tf_op jit(solution)/shard_map/squeeze | solution.py:310
  25.0 0.1 collective-permute-done.halo_ref
  25.1 0.0 copy-start
  25.1 0.9 copy-done
  26.0 30.4 %shard_map.109.x_ref = bf16[2048,1024]{1,0:T(8,128)(2,1)} custom-call(bf16[3,2048,1024]{2,1,0:T(8,128)(2,1)} %bitcast.40, bf16[3,144,1024]{2,1,0:T(8,128)(2,1)} %copy-done, f32[3,7,1024]{2,1,0:T(8,128)} %bitcast.41, f32[64,256]{1,0:T(8,128)} %maximum_maximum_fusion.rows_ref, bf16[2048,1024]{1,0:T(8,128)(2,1)} %get-tuple-element.6.gate_ref), custom_call_target="tpu_custom_call" | custom-call | tf_op jit(solution)/shard_map/pallas_call | solution.py:284
  56.4 9.9 %shard_map.110 = f32[16,1024]{1,0:T(8,128)} custom-call(bf16[2048,1024]{1,0:T(8,128)(2,1)} %shard_map.109.x_ref, bf16[128,512]{1,0:T(8,128)(2,1)} %constant.33.clone.mom_ref, f32[8,16,1024]{2,1,0:T(8,128)} %get-tuple-element.7.cs_ref, f32[16,1024]{1,0:T(8,128)} %get-tuple-element.11.l16_ref), custom_call_target="tpu_custom_call" | custom-call | tf_op jit(solution)/shard_map/pallas_call | solution.py:182
  66.2 4.4 %collective-permute-start.1 = (f32[16,1024]{1,0:T(8,128)}, f32[16,1024]{1,0:T(8,128)S(1)}, u32[]{:S(2)}, u32[]{:S(2)}) collective-permute-start(f32[16,1024]{1,0:T(8,128)} %shard_map.110), channel_id=1, source_target_pairs={{0,4},{4,8},{8,12},{1,5},{5,9},{9,13},{2,6},{6,10},{10,14},{3,7},{... | collective-permute-start | bytes 196616 | tf_op jit(solution)/shard_map/ppermute | solution.py:21
  70.6 4.5 %collective-permute-start.2 = (f32[16,1024]{1,0:T(8,128)}, f32[16,1024]{1,0:T(8,128)S(1)}, u32[]{:S(2)}, u32[]{:S(2)}) collective-permute-start(f32[16,1024]{1,0:T(8,128)} %shard_map.110), channel_id=1, source_target_pairs={{0,8},{4,12},{1,9},{5,13},{2,10},{6,14},{3,11},{7,15},{16,24},{20,... | collective-permute-start | bytes 196616 | tf_op jit(solution)/shard_map/ppermute | solution.py:21
  75.1 1.3 %collective-permute-start.3 = (f32[16,1024]{1,0:T(8,128)}, f32[16,1024]{1,0:T(8,128)S(1)}, u32[]{:S(2)}, u32[]{:S(2)}) collective-permute-start(f32[16,1024]{1,0:T(8,128)} %shard_map.110), channel_id=1, source_target_pairs={{0,12},{1,13},{2,14},{3,15},{16,28},{17,29},{18,30},{19,31}} | collective-permute-start | bytes 196616 | tf_op jit(solution)/shard_map/ppermute | solution.py:21
  76.4 0.0 collective-permute-done.1
  76.4 0.9 collective-permute-done.2
  77.3 1.3 %collective-permute-done.3 = f32[16,1024]{1,0:T(8,128)S(1)} collective-permute-done((f32[16,1024]{1,0:T(8,128)}, f32[16,1024]{1,0:T(8,128)S(1)}, u32[]{:S(2)}, u32[]{:S(2)}) %collective-permute-start.3) | collective-permute-done | bytes 65568 | tf_op jit(solution)/shard_map/ppermute | solution.py:21
  78.6 0.7 fusion
  79.3 1.4 %divide_multiply_fusion.inter_ref = f32[16,8,1024]{2,1,0:T(8,128)} fusion(f32[8]{0:T(128)S(1)} %bitcast.44, f32[16,1024]{1,0:T(8,128)S(1)} %get-tuple-element.12, f32[16,1024]{1,0:T(8,128)S(1)} %get-tuple-element.10), kind=kLoop, calls=%fused_computation.3 | loop fusion | flops 262144 | bytes 655392 | tf_op jit(solution)/shard_map/mul | solution.py:173
  80.7 30.6 %shard_map.111 = bf16[2048,1024]{1,0:T(8,128)(2,1)} custom-call(bf16[2048,1024]{1,0:T(8,128)(2,1)} %shard_map.109.x_ref, bf16[2048,1024]{1,0:T(8,128)(2,1)} %get-tuple-element.5.gate_ref, bf16[1024,256]{1,0:T(8,128)(2,1)} %constant.10.clone.phi_ref, bf16[64,256]{1,0:T(8,128)(2,1)} %constant.11.clone.mom_ref, bf16[128,192]{1,0:T(8,128)(2,1)} %constant.32.clone.psi_ref, ...), custom_call_target="tpu_custom_call" | custom-call | tf_op jit(solution)/shard_map/pallas_call | solution.py:203
  (4 shorter events, 0.0 us)
Async XLA Ops:
  1.2 23.9 %collective-permute-start = (bf16[3,144,1024]{2,1,0:T(8,128)(2,1)S(1)}, bf16[3,144,1024]{2,1,0:T(8,128)(2,1)S(1)}, u32[]{:S(2)}, u32[]{:S(2)}) collective-permute-start(bf16[3,144,1024]{2,1,0:T(8,128)(2,1)S(1)} %slice.12), channel_id=1, source_target_pairs={{0,4},{4,8},{8,12},{1,5},{5,9},{9,13},{2,6},{6,10},{10,14},{3,7},{... | collective-permute-start | bytes 2654216 | tf_op jit(solution)/shard_map/ppermute | solution.py:21
  6.3 9.4 %copy-start.3 = (bf16[64,128]{1,0:T(8,128)(2,1)S(1)}, bf16[64,128]{1,0:T(8,128)(2,1)}, u32[]{:S(2)}) copy-start(bf16[64,128]{1,0:T(8,128)(2,1)} %param.13) | copy-start | bytes 49156
  6.3 9.6 %copy-start.1 = (f32[1024,16]{0,1:T(8,128)S(1)}, f32[1024,16]{0,1:T(8,128)}, u32[]{:S(2)}) copy-start(f32[1024,16]{0,1:T(8,128)} %param.15) | copy-start | bytes 196612
  6.3 9.5 %copy-start.2 = (f32[1024,16]{0,1:T(8,128)S(1)}, f32[1024,16]{0,1:T(8,128)}, u32[]{:S(2)}) copy-start(f32[1024,16]{0,1:T(8,128)} %param.16) | copy-start | bytes 196612
  25.1 0.9 copy-start
  66.2 10.2 %collective-permute-start.1 = (f32[16,1024]{1,0:T(8,128)}, f32[16,1024]{1,0:T(8,128)S(1)}, u32[]{:S(2)}, u32[]{:S(2)}) collective-permute-start(f32[16,1024]{1,0:T(8,128)} %shard_map.110), channel_id=1, source_target_pairs={{0,4},{4,8},{8,12},{1,5},{5,9},{9,13},{2,6},{6,10},{10,14},{3,7},{... | collective-permute-start | bytes 196616 | tf_op jit(solution)/shard_map/ppermute | solution.py:21
  70.6 6.7 %collective-permute-start.2 = (f32[16,1024]{1,0:T(8,128)}, f32[16,1024]{1,0:T(8,128)S(1)}, u32[]{:S(2)}, u32[]{:S(2)}) collective-permute-start(f32[16,1024]{1,0:T(8,128)} %shard_map.110), channel_id=1, source_target_pairs={{0,8},{4,12},{1,9},{5,13},{2,10},{6,14},{3,11},{7,15},{16,24},{20,... | collective-permute-start | bytes 196616 | tf_op jit(solution)/shard_map/ppermute | solution.py:21
  75.1 3.5 %collective-permute-start.3 = (f32[16,1024]{1,0:T(8,128)}, f32[16,1024]{1,0:T(8,128)S(1)}, u32[]{:S(2)}, u32[]{:S(2)}) collective-permute-start(f32[16,1024]{1,0:T(8,128)} %shard_map.110), channel_id=1, source_target_pairs={{0,12},{1,13},{2,14},{3,15},{16,28},{17,29},{18,30},{19,31}} | collective-permute-start | bytes 196616 | tf_op jit(solution)/shard_map/ppermute | solution.py:21
